TPU v7x, 32 devices: a whole 2x2x4 slice. The times are simulated.
32 devices in a mesh: cell: 8 (over y, x, core), gene: 4 (over z).
Axes of the slice: x: 2, y: 2, z: 4, core: 2. Of those that a mesh axis runs over, the one named last changes fastest.
Arguments:
- expression: float32 [12288, 32768], P('cell', 'gene'), may hold values from -16 to 18, as said below
- tile_mask: int32 [48, 128], P('cell', 'gene'), may hold values from 0 to 1, as said below
- start: float32 [32768, 32], P('gene'), may hold values from -6 to 6
Outputs:
- alphas: float32 [2, 32, 32], replicated
- betas: float32 [2, 32, 32], replicated
- next_block: float32 [32768, 32], P('gene')
Inputs may be any that keep to these rules, and one draw needn't show every extreme that they name: expression: positive mean per gene with gene and cell scales and independent noise. `tile_mask`: each row of tiles belongs to one of 8 cell types and each column of tiles to one of 8 gene modules; a tile is 1 where its type expresses its module.
All inputs are finite; a program needn't handle non-finite values.
Results may differ from a plain program's by a relative error of at most 0.0024.
Values sent between devices are 32-bit elements; how exact they have to be, the bound alone decides.
No kernel may reach another device: no remote copies, remote signals or barrier semaphores. Data moves between devices by JAX's collectives and lax.ppermute only.
A program may use at most 256 MiB of HBM per device.

v0:
```python
import math

import jax
import jax.numpy as jnp
from jax import lax
from jax.experimental import pallas as pl
from jax.experimental.pallas import tpu as pltpu
from jax.sharding import PartitionSpec as P

TILE = 256
STEPS = 2
BF = jnp.bfloat16
F32 = jnp.float32


def split(x):
    p1 = x.astype(BF)
    r1 = x - p1.astype(F32)
    p2 = r1.astype(BF)
    p3 = (r1 - p2.astype(F32)).astype(BF)
    return p1, p2, p3


def split_outside(x):
    pieces = []
    rest = x
    for _ in range(2):
        t = rest * 65537.0
        head = t - (t - rest)
        pieces.append(head.astype(BF))
        rest = rest - head
    pieces.append(rest.astype(BF))
    return pieces


def stacks(p, axis):
    return (jnp.concatenate(p, axis=axis), jnp.concatenate(p[:2], axis=axis), p[0])


def butterfly_sum(x, axis):
    n = lax.axis_size(axis)
    if n & (n - 1):
        return lax.psum(x, axis)
    s = 1
    while s < n:
        x = x + lax.ppermute(x, axis, [(i, i ^ s) for i in range(n)])
        s *= 2
    return x


def halving_sum(x, axis, dim):
    n = lax.axis_size(axis)
    if n & (n - 1) or x.shape[dim] % n:
        return lax.psum(x, axis)
    me = lax.axis_index(axis)
    s = 1
    bits = []
    while s < n:
        half = x.shape[dim] // 2
        bit = (me // s) % 2
        keep = lax.dynamic_slice_in_dim(x, bit * half, half, axis=dim)
        send = lax.dynamic_slice_in_dim(x, (1 - bit) * half, half, axis=dim)
        x = keep + lax.ppermute(send, axis, [(i, i ^ s) for i in range(n)])
        bits.append((s, bit))
        s *= 2
    for s, bit in reversed(bits):
        other = lax.ppermute(x, axis, [(i, i ^ s) for i in range(n)])
        lo_first = jnp.concatenate([x, other], axis=dim)
        hi_first = jnp.concatenate([other, x], axis=dim)
        x = jnp.where(bit == 0, lo_first, hi_first)
    return x


def _nt(a, b):
    return lax.dot_general(a, b, (((1,), (1,)), ((), ())), preferred_element_type=F32)


def forward_kernel(x_ref, m_ref, s3_ref, s2_ref, s1_ref, y_ref, *col):
    j = pl.program_id(1)
    k = s1_ref.shape[0]
    x = x_ref[...] * m_ref[0]
    x1, x2, x3 = split(x)
    a = _nt(x1, s3_ref[...])
    c = _nt(x2, s2_ref[...])
    d = _nt(x3, s1_ref[...])
    part = ((a[:, 2 * k:] + c[:, k:] + d) + (a[:, k:2 * k] + c[:, :k])) + a[:, :k]

    @pl.when(j == 0)
    def _():
        y_ref[...] = part

    @pl.when(j > 0)
    def _():
        y_ref[...] += part

    if col:
        (c_ref,) = col
        i = pl.program_id(0)
        tw = x_ref.shape[1]
        s = jnp.sum(x, axis=0, keepdims=True)
        sl = pl.ds(pl.multiple_of(j * tw, tw), tw)

        @pl.when(i == 0)
        def _():
            c_ref[:, sl] = s

        @pl.when(i > 0)
        def _():
            c_ref[:, sl] += s


def backward_kernel(x_ref, m_ref, s3_ref, s2_ref, s1_ref, o_ref):
    i = pl.program_id(1)
    k = s1_ref.shape[0]
    x = x_ref[...] * m_ref[0]
    x1, x2, x3 = split(x)
    a = jnp.dot(s3_ref[...], x1, preferred_element_type=F32)
    c = jnp.dot(s2_ref[...], x2, preferred_element_type=F32)
    d = jnp.dot(s1_ref[...], x3, preferred_element_type=F32)
    part = ((a[2 * k:] + c[k:] + d) + (a[k:2 * k] + c[:k])) + a[:k]

    @pl.when(i == 0)
    def _():
        o_ref[...] = part

    @pl.when(i > 0)
    def _():
        o_ref[...] += part


def blocks(rows, width):
    tr = TILE
    tw = min(width, 4096)
    return tr, tw


def forward(expression, mexp, bt, with_colsum):
    rows, width = expression.shape
    k = bt.shape[0]
    tr, tw = blocks(rows, width)
    s3, s2, s1 = stacks(split_outside(bt), 0)
    in_specs = [
        pl.BlockSpec((tr, tw), lambda i, j: (i, j)),
        pl.BlockSpec((1, 1, tw), lambda i, j: (i, 0, j)),
        pl.BlockSpec((3 * k, tw), lambda i, j: (0, j)),
        pl.BlockSpec((2 * k, tw), lambda i, j: (0, j)),
        pl.BlockSpec((k, tw), lambda i, j: (0, j)),
    ]
    out_specs = [pl.BlockSpec((tr, k), lambda i, j: (i, 0))]
    out_shape = [jax.ShapeDtypeStruct((rows, k), F32)]
    if with_colsum:
        out_specs.append(pl.BlockSpec((1, width), lambda i, j: (0, 0)))
        out_shape.append(jax.ShapeDtypeStruct((1, width), F32))
    return pl.pallas_call(
        forward_kernel,
        grid=(rows // tr, width // tw),
        in_specs=in_specs,
        out_specs=out_specs,
        out_shape=out_shape,
        compiler_params=pltpu.CompilerParams(dimension_semantics=("arbitrary", "arbitrary")),
    )(expression, mexp, s3, s2, s1)


def backward(expression, mexp, y):
    rows, width = expression.shape
    k = y.shape[1]
    tr, tw = blocks(rows, width)
    s3, s2, s1 = stacks(split_outside(jnp.transpose(y)), 0)
    return pl.pallas_call(
        backward_kernel,
        grid=(width // tw, rows // tr),
        in_specs=[
            pl.BlockSpec((tr, tw), lambda j, i: (i, j)),
            pl.BlockSpec((1, 1, tw), lambda j, i: (i, 0, j)),
            pl.BlockSpec((3 * k, tr), lambda j, i: (0, i)),
            pl.BlockSpec((2 * k, tr), lambda j, i: (0, i)),
            pl.BlockSpec((k, tr), lambda j, i: (0, i)),
        ],
        out_specs=pl.BlockSpec((k, tw), lambda j, i: (0, j)),
        out_shape=jax.ShapeDtypeStruct((k, width), F32),
        compiler_params=pltpu.CompilerParams(dimension_semantics=("arbitrary", "arbitrary")),
    )(expression, mexp, s3, s2, s1)


HI = lax.Precision.HIGHEST


def row_gram(a, b):
    return lax.dot_general(a, b, (((1,), (1,)), ((), ())), precision=HI, preferred_element_type=F32)


def left_solve(lower, x):
    return lax.linalg.triangular_solve(lower, x, left_side=True, lower=True)


def right_solve(lower, x):
    return lax.linalg.triangular_solve(lower, x, left_side=False, lower=True, transpose_a=True)


def per_device(expression, tile_mask, start):
    cell_count = lax.axis_size("cell")
    gene_count = lax.axis_size("gene")
    rows, width = expression.shape
    cells = rows * cell_count

    mexp = jnp.repeat(tile_mask.astype(F32), TILE, axis=1)[:, None, :]
    start_t = jnp.transpose(start)
    gram0 = butterfly_sum(row_gram(start_t, start_t), "gene")
    lower0 = jnp.linalg.cholesky(gram0)
    current = left_solve(lower0, start_t)

    y_start, colsum = forward(expression, mexp, start_t, True)
    means = butterfly_sum(colsum[0], "cell") / cells
    y = right_solve(lower0, butterfly_sum(y_start, "gene"))

    older = None
    alpha_list = []
    beta_list = []
    for step in range(STEPS):
        if step > 0:
            y = butterfly_sum(forward(expression, mexp, current, False)[0], "gene")
        mean_side = butterfly_sum(jnp.dot(current, means, precision=HI), "gene")
        raw = halving_sum(backward(expression, mexp, y), "cell", 1)
        image = raw / cells - mean_side[:, None] * means[None, :]
        proj = [row_gram(current, image)]
        if older is not None:
            proj.append(row_gram(older, image))
        summed = butterfly_sum(jnp.stack(proj), "gene")
        resid = image - jnp.dot(jnp.transpose(summed[0]), current, precision=HI)
        if older is not None:
            resid = resid - jnp.dot(jnp.transpose(summed[1]), older, precision=HI)
        g = butterfly_sum(row_gram(resid, resid), "gene")
        lower = jnp.linalg.cholesky(g)
        fresh = left_solve(lower, resid)
        alpha_list.append(summed[0])
        beta_list.append(jnp.transpose(lower))
        older = current
        current = fresh
    next_block = jnp.transpose(current) * math.sqrt(width * gene_count)
    return (jnp.stack(alpha_list), jnp.stack(beta_list), next_block)


def solution(mesh):
    in_specs = (P("cell", "gene"), P("cell", "gene"), P("gene", None))
    out_specs = (P(), P(), P("gene", None))
    return jax.shard_map(
        per_device, mesh=mesh, in_specs=in_specs, out_specs=out_specs, check_vma=False
    )
```

profile of v0, /device:TPU:0, one launch (start us, length us, event | category | flops | bytes accessed | tf_op | source)
XLA Modules:
  0.0 311.4 jit_solution(11309800877815986094)
XLA Ops:
  3.3 3.1 collective-permute-start
  8.1 3.0 collective-permute-start.1
  13.2 32.3 %shard_map.58 = (f32[1536,32]{1,0:T(8,128)}, f32[1,8192]{1,0:T(1,128)}) custom-call(f32[1536,8192]{1,0:T(8,128)} %x_ref.7, f32[6,1,8192]{2,1,0:T(1,128)} %broadcast_in_dim_reshape.3.m_ref, bf16[96,8192]{1,0:T(8,128)(2,1)} %pad_maximum_fusion.s3_ref, bf16[64,8192]{1,0:T(8,128)(2,1)} %pad_maximum_fusion.2.s2_ref, bf16[32,8192]{1,0:T(8,128)(2,1)} %copy-done.1), custom_call_target="tpu_custom_call" | custom-call | tf_op jit(solution)/shard_map/pallas_call | solution.py:154
  48.7 2.9 cholesky.59
  56.7 6.2 %collective-permute-done.3 = f32[1536,32]{0,1:T(8,128)S(1)} collective-permute-done((f32[1536,32]{0,1:T(8,128)S(1)}, f32[1536,32]{0,1:T(8,128)S(1)}, u32[]{:S(2)}, u32[]{:S(2)}) %collective-permute-start.3) | collective-permute-done | bytes 196640 | tf_op jit(solution)/shard_map/ppermute | solution.py:46
  65.6 26.0 %shard_map.59 = f32[32,8192]{1,0:T(8,128)} custom-call(f32[1536,8192]{1,0:T(8,128)} %x_ref.7, f32[6,1,8192]{2,1,0:T(1,128)} %broadcast_in_dim_reshape.3.m_ref, bf16[96,1536]{1,0:T(8,128)(2,1)} %pad_maximum_fusion.4.s3_ref, bf16[64,1536]{1,0:T(8,128)(2,1)} %pad_maximum_fusion.6.s2_ref, bf16[32,1536]{1,0:T(8,128)(2,1)} %copy-done.5), custom_call_target="tpu_custom_call" | custom-call | tf_op jit(solution)/shard_map/pallas_call | solution.py:169
  97.4 6.9 %collective-permute-done.5 = f32[32,2048]{1,0:T(8,128)S(1)} collective-permute-done((f32[32,2048]{1,0:T(8,128)S(1)}, f32[32,2048]{1,0:T(8,128)S(1)}, u32[]{:S(2)}, u32[]{:S(2)}) %collective-permute-start.5) | collective-permute-done | bytes 262176 | tf_op jit(solution)/shard_map/ppermute | solution.py:63
  105.9 3.5 %collective-permute-done.6 = f32[32,1024]{1,0:T(8,128)S(1)} collective-permute-done((f32[32,1024]{1,0:T(8,128)S(1)}, f32[32,1024]{1,0:T(8,128)S(1)}, u32[]{:S(2)}, u32[]{:S(2)}) %collective-permute-start.6) | collective-permute-done | bytes 131104 | tf_op jit(solution)/shard_map/ppermute | solution.py:63
  111.0 3.5 %collective-permute-done.7 = f32[32,1024]{1,0:T(8,128)S(1)} collective-permute-done((f32[32,1024]{1,0:T(8,128)S(1)}, f32[32,1024]{1,0:T(8,128)S(1)}, u32[]{:S(2)}, u32[]{:S(2)}) %collective-permute-start.7) | collective-permute-done | bytes 131104 | tf_op jit(solution)/shard_map/ppermute | solution.py:67
  117.8 3.8 %collective-permute-done.11 = f32[8192]{0:T(1024)S(1)} collective-permute-done((f32[8192]{0:T(1024)S(1)}, f32[8192]{0:T(1024)S(1)}, u32[]{:S(2)}, u32[]{:S(2)}) %collective-permute-start.11) | collective-permute-done | bytes 32800 | tf_op jit(solution)/shard_map/ppermute | solution.py:46
  126.4 3.6 %collective-permute-done.13 = f32[32]{0:T(128)S(1)} collective-permute-done((f32[32]{0:T(128)S(1)}, f32[32]{0:T(128)S(1)}, u32[]{:S(2)}, u32[]{:S(2)}) %collective-permute-start.13) | collective-permute-done | bytes 160 | tf_op jit(solution)/shard_map/ppermute | solution.py:46
  130.0 4.4 %collective-permute-done.14 = f32[32]{0:T(128)S(1)} collective-permute-done((f32[32]{0:T(128)S(1)}, f32[32]{0:T(128)S(1)}, u32[]{:S(2)}, u32[]{:S(2)}) %collective-permute-start.14) | collective-permute-done | bytes 160 | tf_op jit(solution)/shard_map/ppermute | solution.py:46
  135.7 3.7 %collective-permute-done.15 = f32[1,32,32]{2,1,0:T(8,128)S(1)} collective-permute-done((f32[1,32,32]{2,1,0:T(8,128)S(1)}, f32[1,32,32]{2,1,0:T(8,128)S(1)}, u32[]{:S(2)}, u32[]{:S(2)}) %collective-permute-start.15) | collective-permute-done | bytes 4128 | tf_op jit(solution)/shard_map/ppermute | solution.py:46
  139.4 4.6 %collective-permute-done.16 = f32[1,32,32]{2,1,0:T(8,128)S(1)} collective-permute-done((f32[1,32,32]{2,1,0:T(8,128)S(1)}, f32[1,32,32]{2,1,0:T(8,128)S(1)}, u32[]{:S(2)}, u32[]{:S(2)}) %collective-permute-start.16) | collective-permute-done | bytes 4128 | tf_op jit(solution)/shard_map/ppermute | solution.py:46
  147.8 3.7 %collective-permute-done.17 = f32[32,32]{0,1:T(8,128)S(1)} collective-permute-done((f32[32,32]{0,1:T(8,128)S(1)}, f32[32,32]{0,1:T(8,128)S(1)}, u32[]{:S(2)}, u32[]{:S(2)}) %collective-permute-start.17) | collective-permute-done | bytes 4128 | tf_op jit(solution)/shard_map/ppermute | solution.py:46
  151.6 4.5 %collective-permute-done.18 = f32[32,32]{0,1:T(8,128)S(1)} collective-permute-done((f32[32,32]{0,1:T(8,128)S(1)}, f32[32,32]{0,1:T(8,128)S(1)}, u32[]{:S(2)}, u32[]{:S(2)}) %collective-permute-start.18) | collective-permute-done | bytes 4128 | tf_op jit(solution)/shard_map/ppermute | solution.py:46
  156.2 2.9 cholesky.70
  166.7 30.7 %shard_map.60 = f32[1536,32]{1,0:T(8,128)} custom-call(f32[1536,8192]{1,0:T(8,128)} %x_ref.7, f32[6,1,8192]{2,1,0:T(1,128)} %broadcast_in_dim_reshape.3.m_ref, bf16[96,8192]{1,0:T(8,128)(2,1)} %pad_maximum_fusion.1.s3_ref, bf16[64,8192]{1,0:T(8,128)(2,1)} %pad_maximum_fusion.3.s2_ref, bf16[32,8192]{1,0:T(8,128)(2,1)} %copy-done.2), custom_call_target="tpu_custom_call" | custom-call | tf_op jit(solution)/shard_map/pallas_call | solution.py:154
  198.8 6.5 %collective-permute-done.19 = f32[1536,32]{0,1:T(8,128)S(1)} collective-permute-done((f32[1536,32]{0,1:T(8,128)S(1)}, f32[1536,32]{0,1:T(8,128)S(1)}, u32[]{:S(2)}, u32[]{:S(2)}) %collective-permute-start.19) | collective-permute-done | bytes 196640 | tf_op jit(solution)/shard_map/ppermute | solution.py:46
  205.5 7.6 %collective-permute-done.20 = f32[1536,32]{0,1:T(8,128)S(1)} collective-permute-done((f32[1536,32]{0,1:T(8,128)S(1)}, f32[1536,32]{0,1:T(8,128)S(1)}, u32[]{:S(2)}, u32[]{:S(2)}) %collective-permute-start.20) | collective-permute-done | bytes 196640 | tf_op jit(solution)/shard_map/ppermute | solution.py:46
  214.7 26.0 %shard_map.61 = f32[32,8192]{1,0:T(8,128)} custom-call(f32[1536,8192]{1,0:T(8,128)} %x_ref.7, f32[6,1,8192]{2,1,0:T(1,128)} %broadcast_in_dim_reshape.3.m_ref, bf16[96,1536]{1,0:T(8,128)(2,1)} %pad_maximum_fusion.5.s3_ref, bf16[64,1536]{1,0:T(8,128)(2,1)} %pad_maximum_fusion.7.s2_ref, bf16[32,1536]{1,0:T(8,128)(2,1)} %copy-done.6), custom_call_target="tpu_custom_call" | custom-call | tf_op jit(solution)/shard_map/pallas_call | solution.py:169
  246.4 6.9 %collective-permute-done.22 = f32[32,2048]{1,0:T(8,128)S(1)} collective-permute-done((f32[32,2048]{1,0:T(8,128)S(1)}, f32[32,2048]{1,0:T(8,128)S(1)}, u32[]{:S(2)}, u32[]{:S(2)}) %collective-permute-start.22) | collective-permute-done | bytes 262176 | tf_op jit(solution)/shard_map/ppermute | solution.py:63
  254.5 3.9 %collective-permute-done.23 = f32[32,1024]{1,0:T(8,128)S(1)} collective-permute-done((f32[32,1024]{1,0:T(8,128)S(1)}, f32[32,1024]{1,0:T(8,128)S(1)}, u32[]{:S(2)}, u32[]{:S(2)}) %collective-permute-start.23) | collective-permute-done | bytes 131104 | tf_op jit(solution)/shard_map/ppermute | solution.py:63
  259.6 3.9 %collective-permute-done.24 = f32[32,1024]{1,0:T(8,128)S(1)} collective-permute-done((f32[32,1024]{1,0:T(8,128)S(1)}, f32[32,1024]{1,0:T(8,128)S(1)}, u32[]{:S(2)}, u32[]{:S(2)}) %collective-permute-start.24) | collective-permute-done | bytes 131104 | tf_op jit(solution)/shard_map/ppermute | solution.py:67
  265.0 4.9 %collective-permute-done.25 = f32[32,2048]{1,0:T(8,128)S(1)} collective-permute-done((f32[32,2048]{1,0:T(8,128)S(1)}, f32[32,2048]{1,0:T(8,128)S(1)}, u32[]{:S(2)}, u32[]{:S(2)}) %collective-permute-start.25) | collective-permute-done | bytes 262176 | tf_op jit(solution)/shard_map/ppermute | solution.py:67
  271.0 3.6 %collective-permute-done.27 = f32[32]{0:T(128)S(1)} collective-permute-done((f32[32]{0:T(128)S(1)}, f32[32]{0:T(128)S(1)}, u32[]{:S(2)}, u32[]{:S(2)}) %collective-permute-start.27) | collective-permute-done | bytes 160 | tf_op jit(solution)/shard_map/ppermute | solution.py:46
  275.0 4.0 %collective-permute-done.28 = f32[32]{0:T(128)S(1)} collective-permute-done((f32[32]{0:T(128)S(1)}, f32[32]{0:T(128)S(1)}, u32[]{:S(2)}, u32[]{:S(2)}) %collective-permute-start.28) | collective-permute-done | bytes 160 | tf_op jit(solution)/shard_map/ppermute | solution.py:46
  281.4 3.9 %collective-permute-done.29 = f32[2,32,32]{2,1,0:T(8,128)S(1)} collective-permute-done((f32[2,32,32]{2,1,0:T(8,128)S(1)}, f32[2,32,32]{2,1,0:T(8,128)S(1)}, u32[]{:S(2)}, u32[]{:S(2)}) %collective-permute-start.29) | collective-permute-done | bytes 8224 | tf_op jit(solution)/shard_map/ppermute | solution.py:46
  285.8 4.4 %collective-permute-done.30 = f32[2,32,32]{2,1,0:T(8,128)S(1)} collective-permute-done((f32[2,32,32]{2,1,0:T(8,128)S(1)}, f32[2,32,32]{2,1,0:T(8,128)S(1)}, u32[]{:S(2)}, u32[]{:S(2)}) %collective-permute-start.30) | collective-permute-done | bytes 8224 | tf_op jit(solution)/shard_map/ppermute | solution.py:46
  293.5 3.7 %collective-permute-done.31 = f32[32,32]{0,1:T(8,128)S(1)} collective-permute-done((f32[32,32]{0,1:T(8,128)S(1)}, f32[32,32]{0,1:T(8,128)S(1)}, u32[]{:S(2)}, u32[]{:S(2)}) %collective-permute-start.31) | collective-permute-done | bytes 4128 | tf_op jit(solution)/shard_map/ppermute | solution.py:46
  298.3 3.6 %collective-permute-done.32 = f32[32,32]{0,1:T(8,128)S(1)} collective-permute-done((f32[32,32]{0,1:T(8,128)S(1)}, f32[32,32]{0,1:T(8,128)S(1)}, u32[]{:S(2)}, u32[]{:S(2)}) %collective-permute-start.32) | collective-permute-done | bytes 4128 | tf_op jit(solution)/shard_map/ppermute | solution.py:46
  302.0 2.9 cholesky.81
  (152 shorter events, 75.2 us)
Async XLA Ops:
  3.3 4.8 %collective-permute-start = (f32[32,32]{0,1:T(8,128)S(1)}, f32[32,32]{0,1:T(8,128)S(1)}, u32[]{:S(2)}, u32[]{:S(2)}) collective-permute-start(f32[32,32]{0,1:T(8,128)S(1)} %fusion.51), channel_id=1, source_target_pairs={{0,1},{1,0},{2,3},{3,2},{4,5},{5,4},{6,7},{7,6},{8,9},{9,8},{10,11... | collective-permute-start | bytes 12296 | tf_op jit(solution)/shard_map/ppermute | solution.py:46
  8.1 40.4 %collective-permute-start.1 = (f32[32,32]{0,1:T(8,128)S(1)}, f32[32,32]{0,1:T(8,128)S(1)}, u32[]{:S(2)}, u32[]{:S(2)}) collective-permute-start(f32[32,32]{0,1:T(8,128)S(1)} %add.131), channel_id=1, source_target_pairs={{0,2},{1,3},{2,0},{3,1},{4,6},{5,7},{6,4},{7,5},{8,10},{9,11},{10,... | collective-permute-start | bytes 12296 | tf_op jit(solution)/shard_map/ppermute | solution.py:46
  46.9 5.7 %collective-permute-start.2 = (f32[1536,32]{0,1:T(8,128)S(1)}, f32[1536,32]{0,1:T(8,128)S(1)}, u32[]{:S(2)}, u32[]{:S(2)}) collective-permute-start(f32[1536,32]{0,1:T(8,128)S(1)} %copy.21), channel_id=1, source_target_pairs={{0,1},{1,0},{2,3},{3,2},{4,5},{5,4},{6,7},{7,6},{8,9},{9,8},{10,11... | collective-permute-start | bytes 589832 | tf_op jit(solution)/shard_map/ppermute | solution.py:46
  53.3 9.7 %collective-permute-start.3 = (f32[1536,32]{0,1:T(8,128)S(1)}, f32[1536,32]{0,1:T(8,128)S(1)}, u32[]{:S(2)}, u32[]{:S(2)}) collective-permute-start(f32[1536,32]{0,1:T(8,128)S(1)} %copy.23), channel_id=1, source_target_pairs={{0,2},{1,3},{2,0},{3,1},{4,6},{5,7},{6,4},{7,5},{8,10},{9,11},{10,... | collective-permute-start | bytes 589832 | tf_op jit(solution)/shard_map/ppermute | solution.py:46
  92.8 2.0 collective-permute-start.4
  95.9 8.4 %collective-permute-start.5 = (f32[32,2048]{1,0:T(8,128)S(1)}, f32[32,2048]{1,0:T(8,128)S(1)}, u32[]{:S(2)}, u32[]{:S(2)}) collective-permute-start(f32[32,2048]{1,0:T(8,128)S(1)} %constant_dynamic-slice_fusion.4), channel_id=1, source_target_pairs={{0,8},{4,12},{8,0},{12,4},{16,24},{20,28},{24,16},{28,20},{1,9},{5... | collective-permute-start | bytes 786440 | tf_op jit(solution)/shard_map/ppermute | solution.py:63
  104.3 5.0 %collective-permute-start.6 = (f32[32,1024]{1,0:T(8,128)S(1)}, f32[32,1024]{1,0:T(8,128)S(1)}, u32[]{:S(2)}, u32[]{:S(2)}) collective-permute-start(f32[32,1024]{1,0:T(8,128)S(1)} %constant_dynamic-slice_fusion.3), channel_id=1, source_target_pairs={{0,16},{4,20},{8,24},{12,28},{16,0},{20,4},{24,8},{28,12},{1,17},{... | collective-permute-start | bytes 393224 | tf_op jit(solution)/shard_map/ppermute | solution.py:63
  109.4 5.0 %collective-permute-start.7 = (f32[32,1024]{1,0:T(8,128)S(1)}, f32[32,1024]{1,0:T(8,128)S(1)}, u32[]{:S(2)}, u32[]{:S(2)}) collective-permute-start(f32[32,1024]{1,0:T(8,128)S(1)} %dynamic-slice_add_fusion.5), channel_id=1, source_target_pairs={{0,16},{4,20},{8,24},{12,28},{16,0},{20,4},{24,8},{28,12},{1,17},{... | collective-permute-start | bytes 393224 | tf_op jit(solution)/shard_map/ppermute | solution.py:67
  114.4 8.7 %collective-permute-start.8 = (f32[32,2048]{1,0:T(8,128)S(1)}, f32[32,2048]{1,0:T(8,128)S(1)}, u32[]{:S(2)}, u32[]{:S(2)}) collective-permute-start(f32[32,2048]{1,0:T(8,128)S(1)} %maximum_select_fusion.4), channel_id=1, source_target_pairs={{0,8},{4,12},{8,0},{12,4},{16,24},{20,28},{24,16},{28,20},{1,9},{5... | collective-permute-start | bytes 786440 | tf_op jit(solution)/shard_map/ppermute | solution.py:67
  117.2 4.4 %collective-permute-start.11 = (f32[8192]{0:T(1024)S(1)}, f32[8192]{0:T(1024)S(1)}, u32[]{:S(2)}, u32[]{:S(2)}) collective-permute-start(f32[8192]{0:T(1024)S(1)} %add.147), channel_id=1, source_target_pairs={{0,8},{4,12},{8,0},{12,4},{16,24},{20,28},{24,16},{28,20},{1,9},{5... | collective-permute-start | bytes 98312 | tf_op jit(solution)/shard_map/ppermute | solution.py:46
  121.6 3.9 %collective-permute-start.12 = (f32[8192]{0:T(1024)S(1)}, f32[8192]{0:T(1024)S(1)}, u32[]{:S(2)}, u32[]{:S(2)}) collective-permute-start(f32[8192]{0:T(1024)S(1)} %add.148), channel_id=1, source_target_pairs={{0,16},{4,20},{8,24},{12,28},{16,0},{20,4},{24,8},{28,12},{1,17},{... | collective-permute-start | bytes 98312 | tf_op jit(solution)/shard_map/ppermute | solution.py:46
  123.2 11.3 %collective-permute-start.9 = (f32[32,4096]{1,0:T(8,128)S(1)}, f32[32,4096]{1,0:T(8,128)S(1)}, u32[]{:S(2)}, u32[]{:S(2)}) collective-permute-start(f32[32,4096]{1,0:T(8,128)S(1)} %maximum_select_fusion.2), channel_id=1, source_target_pairs={{0,4},{4,0},{8,12},{12,8},{16,20},{20,16},{24,28},{28,24},{1,5},{5... | collective-permute-start | bytes 1572872 | tf_op jit(solution)/shard_map/ppermute | solution.py:67
  126.4 3.6 %collective-permute-start.13 = (f32[32]{0:T(128)S(1)}, f32[32]{0:T(128)S(1)}, u32[]{:S(2)}, u32[]{:S(2)}) collective-permute-start(f32[32]{0:T(128)S(1)} %convolution_bitcast_fusion.4), channel_id=1, source_target_pairs={{0,1},{1,0},{2,3},{3,2},{4,5},{5,4},{6,7},{7,6},{8,9},{9,8},{10,11... | collective-permute-start | bytes 392 | tf_op jit(solution)/shard_map/ppermute | solution.py:46
  130.0 4.4 %collective-permute-start.14 = (f32[32]{0:T(128)S(1)}, f32[32]{0:T(128)S(1)}, u32[]{:S(2)}, u32[]{:S(2)}) collective-permute-start(f32[32]{0:T(128)S(1)} %add.150), channel_id=1, source_target_pairs={{0,2},{1,3},{2,0},{3,1},{4,6},{5,7},{6,4},{7,5},{8,10},{9,11},{10,... | collective-permute-start | bytes 392 | tf_op jit(solution)/shard_map/ppermute | solution.py:46
  135.6 3.8 %collective-permute-start.15 = (f32[1,32,32]{2,1,0:T(8,128)S(1)}, f32[1,32,32]{2,1,0:T(8,128)S(1)}, u32[]{:S(2)}, u32[]{:S(2)}) collective-permute-start(f32[1,32,32]{2,1,0:T(8,128)S(1)} %convolution_bitcast_fusion.2), channel_id=1, source_target_pairs={{0,1},{1,0},{2,3},{3,2},{4,5},{5,4},{6,7},{7,6},{8,9},{9,8},{10,11... | collective-permute-start | bytes 12296 | tf_op jit(solution)/shard_map/ppermute | solution.py:46
  139.4 4.6 %collective-permute-start.16 = (f32[1,32,32]{2,1,0:T(8,128)S(1)}, f32[1,32,32]{2,1,0:T(8,128)S(1)}, u32[]{:S(2)}, u32[]{:S(2)}) collective-permute-start(f32[1,32,32]{2,1,0:T(8,128)S(1)} %add.152), channel_id=1, source_target_pairs={{0,2},{1,3},{2,0},{3,1},{4,6},{5,7},{6,4},{7,5},{8,10},{9,11},{10,... | collective-permute-start | bytes 12296 | tf_op jit(solution)/shard_map/ppermute | solution.py:46
  147.7 3.8 %collective-permute-start.17 = (f32[32,32]{0,1:T(8,128)S(1)}, f32[32,32]{0,1:T(8,128)S(1)}, u32[]{:S(2)}, u32[]{:S(2)}) collective-permute-start(f32[32,32]{0,1:T(8,128)S(1)} %fusion.52), channel_id=1, source_target_pairs={{0,1},{1,0},{2,3},{3,2},{4,5},{5,4},{6,7},{7,6},{8,9},{9,8},{10,11... | collective-permute-start | bytes 12296 | tf_op jit(solution)/shard_map/ppermute | solution.py:46
  151.5 4.6 %collective-permute-start.18 = (f32[32,32]{0,1:T(8,128)S(1)}, f32[32,32]{0,1:T(8,128)S(1)}, u32[]{:S(2)}, u32[]{:S(2)}) collective-permute-start(f32[32,32]{0,1:T(8,128)S(1)} %add.154), channel_id=1, source_target_pairs={{0,2},{1,3},{2,0},{3,1},{4,6},{5,7},{6,4},{7,5},{8,10},{9,11},{10,... | collective-permute-start | bytes 12296 | tf_op jit(solution)/shard_map/ppermute | solution.py:46
  198.8 6.6 %collective-permute-start.19 = (f32[1536,32]{0,1:T(8,128)S(1)}, f32[1536,32]{0,1:T(8,128)S(1)}, u32[]{:S(2)}, u32[]{:S(2)}) collective-permute-start(f32[1536,32]{0,1:T(8,128)S(1)} %copy.29), channel_id=1, source_target_pairs={{0,1},{1,0},{2,3},{3,2},{4,5},{5,4},{6,7},{7,6},{8,9},{9,8},{10,11... | collective-permute-start | bytes 589832 | tf_op jit(solution)/shard_map/ppermute | solution.py:46
  205.4 7.7 %collective-permute-start.20 = (f32[1536,32]{0,1:T(8,128)S(1)}, f32[1536,32]{0,1:T(8,128)S(1)}, u32[]{:S(2)}, u32[]{:S(2)}) collective-permute-start(f32[1536,32]{0,1:T(8,128)S(1)} %add.156), channel_id=1, source_target_pairs={{0,2},{1,3},{2,0},{3,1},{4,6},{5,7},{6,4},{7,5},{8,10},{9,11},{10,... | collective-permute-start | bytes 589832 | tf_op jit(solution)/shard_map/ppermute | solution.py:46
  241.8 2.0 collective-permute-start.21
  244.9 8.4 %collective-permute-start.22 = (f32[32,2048]{1,0:T(8,128)S(1)}, f32[32,2048]{1,0:T(8,128)S(1)}, u32[]{:S(2)}, u32[]{:S(2)}) collective-permute-start(f32[32,2048]{1,0:T(8,128)S(1)} %constant_dynamic-slice_fusion.1), channel_id=1, source_target_pairs={{0,8},{4,12},{8,0},{12,4},{16,24},{20,28},{24,16},{28,20},{1,9},{5... | collective-permute-start | bytes 786440 | tf_op jit(solution)/shard_map/ppermute | solution.py:63
  253.4 5.0 %collective-permute-start.23 = (f32[32,1024]{1,0:T(8,128)S(1)}, f32[32,1024]{1,0:T(8,128)S(1)}, u32[]{:S(2)}, u32[]{:S(2)}) collective-permute-start(f32[32,1024]{1,0:T(8,128)S(1)} %constant_dynamic-slice_fusion), channel_id=1, source_target_pairs={{0,16},{4,20},{8,24},{12,28},{16,0},{20,4},{24,8},{28,12},{1,17},{... | collective-permute-start | bytes 393224 | tf_op jit(solution)/shard_map/ppermute | solution.py:63
  258.4 5.0 %collective-permute-start.24 = (f32[32,1024]{1,0:T(8,128)S(1)}, f32[32,1024]{1,0:T(8,128)S(1)}, u32[]{:S(2)}, u32[]{:S(2)}) collective-permute-start(f32[32,1024]{1,0:T(8,128)S(1)} %dynamic-slice_add_fusion.4), channel_id=1, source_target_pairs={{0,16},{4,20},{8,24},{12,28},{16,0},{20,4},{24,8},{28,12},{1,17},{... | collective-permute-start | bytes 393224 | tf_op jit(solution)/shard_map/ppermute | solution.py:67
  263.5 6.4 %collective-permute-start.25 = (f32[32,2048]{1,0:T(8,128)S(1)}, f32[32,2048]{1,0:T(8,128)S(1)}, u32[]{:S(2)}, u32[]{:S(2)}) collective-permute-start(f32[32,2048]{1,0:T(8,128)S(1)} %maximum_select_fusion.5), channel_id=1, source_target_pairs={{0,8},{4,12},{8,0},{12,4},{16,24},{20,28},{24,16},{28,20},{1,9},{5... | collective-permute-start | bytes 786440 | tf_op jit(solution)/shard_map/ppermute | solution.py:67
  270.0 9.0 %collective-permute-start.26 = (f32[32,4096]{1,0:T(8,128)S(1)}, f32[32,4096]{1,0:T(8,128)S(1)}, u32[]{:S(2)}, u32[]{:S(2)}) collective-permute-start(f32[32,4096]{1,0:T(8,128)S(1)} %maximum_select_fusion.3), channel_id=1, source_target_pairs={{0,4},{4,0},{8,12},{12,8},{16,20},{20,16},{24,28},{28,24},{1,5},{5... | collective-permute-start | bytes 1572872 | tf_op jit(solution)/shard_map/ppermute | solution.py:67
  271.0 3.6 %collective-permute-start.27 = (f32[32]{0:T(128)S(1)}, f32[32]{0:T(128)S(1)}, u32[]{:S(2)}, u32[]{:S(2)}) collective-permute-start(f32[32]{0:T(128)S(1)} %convolution_bitcast_fusion.3), channel_id=1, source_target_pairs={{0,1},{1,0},{2,3},{3,2},{4,5},{5,4},{6,7},{7,6},{8,9},{9,8},{10,11... | collective-permute-start | bytes 392 | tf_op jit(solution)/shard_map/ppermute | solution.py:46
  274.5 4.4 %collective-permute-start.28 = (f32[32]{0:T(128)S(1)}, f32[32]{0:T(128)S(1)}, u32[]{:S(2)}, u32[]{:S(2)}) collective-permute-start(f32[32]{0:T(128)S(1)} %add.161), channel_id=1, source_target_pairs={{0,2},{1,3},{2,0},{3,1},{4,6},{5,7},{6,4},{7,5},{8,10},{9,11},{10,... | collective-permute-start | bytes 392 | tf_op jit(solution)/shard_map/ppermute | solution.py:46
  281.3 4.0 %collective-permute-start.29 = (f32[2,32,32]{2,1,0:T(8,128)S(1)}, f32[2,32,32]{2,1,0:T(8,128)S(1)}, u32[]{:S(2)}, u32[]{:S(2)}) collective-permute-start(f32[2,32,32]{2,1,0:T(8,128)S(1)} %pad_maximum_fusion.8), channel_id=1, source_target_pairs={{0,1},{1,0},{2,3},{3,2},{4,5},{5,4},{6,7},{7,6},{8,9},{9,8},{10,11... | collective-permute-start | bytes 24584 | tf_op jit(solution)/shard_map/ppermute | solution.py:46
  285.3 4.9 %collective-permute-start.30 = (f32[2,32,32]{2,1,0:T(8,128)S(1)}, f32[2,32,32]{2,1,0:T(8,128)S(1)}, u32[]{:S(2)}, u32[]{:S(2)}) collective-permute-start(f32[2,32,32]{2,1,0:T(8,128)S(1)} %fusion.48), channel_id=1, source_target_pairs={{0,2},{1,3},{2,0},{3,1},{4,6},{5,7},{6,4},{7,5},{8,10},{9,11},{10,... | collective-permute-start | bytes 24584 | tf_op jit(solution)/shard_map/ppermute | solution.py:46
  293.4 3.8 %collective-permute-start.31 = (f32[32,32]{0,1:T(8,128)S(1)}, f32[32,32]{0,1:T(8,128)S(1)}, u32[]{:S(2)}, u32[]{:S(2)}) collective-permute-start(f32[32,32]{0,1:T(8,128)S(1)} %fusion.53), channel_id=1, source_target_pairs={{0,1},{1,0},{2,3},{3,2},{4,5},{5,4},{6,7},{7,6},{8,9},{9,8},{10,11... | collective-permute-start | bytes 12296 | tf_op jit(solution)/shard_map/ppermute | solution.py:46
  297.2 4.6 %collective-permute-start.32 = (f32[32,32]{0,1:T(8,128)S(1)}, f32[32,32]{0,1:T(8,128)S(1)}, u32[]{:S(2)}, u32[]{:S(2)}) collective-permute-start(f32[32,32]{0,1:T(8,128)S(1)} %add.165), channel_id=1, source_target_pairs={{0,2},{1,3},{2,0},{3,1},{4,6},{5,7},{6,4},{7,5},{8,10},{9,11},{10,... | collective-permute-start | bytes 12296 | tf_op jit(solution)/shard_map/ppermute | solution.py:46
  (11 other events, 74.7 us)
where the time goes:
time: 312 us; the launch traced here: 311 us
  Pallas kernels  115 us (37%)
  waiting for transfers between devices  112 us (36%)
  other arithmetic  31.3 us (10%)
  starting transfers between devices  24.1 us (8%)
  matrix products  20.2 us (6%)
  local copies, waits for them, and re-layouts  7.78 us (2%)
    ppermute x21, waiting for transfers between devices, butterfly_sum(): x = x + lax.ppermute(x, axis, [(i, i ^ s) for i in range(n)])  74.8 us
    pallas_call x2, Pallas kernels, forward(): pl.pallas_call(forward_kernel, grid=(rows // tr, width // tw), in_specs=i...  63 us
    pallas_call x2, Pallas kernels, backward(): pl.pallas_call(backward_kernel, grid=(width // tw, rows // tr), in_specs=...  52.1 us
    ppermute x6, waiting for transfers between devices, halving_sum(): x = keep + lax.ppermute(send, axis, [(i, i ^ s) for i in range(n)])  24.8 us
    ppermute x6, waiting for transfers between devices, halving_sum(): other = lax.ppermute(x, axis, [(i, i ^ s) for i in range(n)])  12.2 us
    ppermute x21, starting transfers between devices, butterfly_sum(): x = x + lax.ppermute(x, axis, [(i, i ^ s) for i in range(n)])  12.2 us
    another operation x5, other arithmetic, left_solve(): return lax.linalg.triangular_solve(lower, x, left_side=True, lower=True)  8.61 us
    dot_general x6, matrix products, row_gram(): lax.dot_general(a, b, (((1,), (1,)), ((), ())), precision=HI, preferred_e...  8.06 us
  transfers between devices with their start and end apart: 33, of which 28 were waited for; matrix products, arithmetic and copies ran while one was open for 5% of the time, Pallas kernels for 10%

commit v1 on v0

--- a/solution.py
+++ b/solution.py
@@ -53,15 +53,19 @@
     if n & (n - 1) or x.shape[dim] % n:
         return lax.psum(x, axis)
     me = lax.axis_index(axis)
+    levels = max(n.bit_length() - 2, 0)
     s = 1
     bits = []
-    while s < n:
+    for _ in range(levels):
         half = x.shape[dim] // 2
         bit = (me // s) % 2
         keep = lax.dynamic_slice_in_dim(x, bit * half, half, axis=dim)
         send = lax.dynamic_slice_in_dim(x, (1 - bit) * half, half, axis=dim)
         x = keep + lax.ppermute(send, axis, [(i, i ^ s) for i in range(n)])
         bits.append((s, bit))
+        s *= 2
+    while s < n:
+        x = x + lax.ppermute(x, axis, [(i, i ^ s) for i in range(n)])
         s *= 2
     for s, bit in reversed(bits):
         other = lax.ppermute(x, axis, [(i, i ^ s) for i in range(n)])
@@ -202,30 +206,33 @@
     gene_count = lax.axis_size("gene")
     rows, width = expression.shape
     cells = rows * cell_count
-
     mexp = jnp.repeat(tile_mask.astype(F32), TILE, axis=1)[:, None, :]
     start_t = jnp.transpose(start)
+
+    y_start, colsum = forward(expression, mexp, start_t, True)
+    start_t = lax.optimization_barrier((start_t, y_start))[0]
     gram0 = butterfly_sum(row_gram(start_t, start_t), "gene")
     lower0 = jnp.linalg.cholesky(gram0)
     current = left_solve(lower0, start_t)
-
-    y_start, colsum = forward(expression, mexp, start_t, True)
     means = butterfly_sum(colsum[0], "cell") / cells
     y = right_solve(lower0, butterfly_sum(y_start, "gene"))
 
     older = None
+    older_side = None
     alpha_list = []
     beta_list = []
     for step in range(STEPS):
         if step > 0:
             y = butterfly_sum(forward(expression, mexp, current, False)[0], "gene")
         mean_side = butterfly_sum(jnp.dot(current, means, precision=HI), "gene")
-        raw = halving_sum(backward(expression, mexp, y), "cell", 1)
+        part = backward(expression, mexp, y)
+        basis = [current] if older is None else [current, older]
+        sides = [mean_side] if older is None else [mean_side, older_side]
+        proj_part = jnp.stack([row_gram(v, part) for v in basis])
+        proj_raw = butterfly_sum(butterfly_sum(proj_part, "cell"), "gene")
+        raw = halving_sum(part, "cell", 1)
         image = raw / cells - mean_side[:, None] * means[None, :]
-        proj = [row_gram(current, image)]
-        if older is not None:
-            proj.append(row_gram(older, image))
-        summed = butterfly_sum(jnp.stack(proj), "gene")
+        summed = [proj_raw[t] / cells - sides[t][:, None] * mean_side[None, :] for t in range(len(basis))]
         resid = image - jnp.dot(jnp.transpose(summed[0]), current, precision=HI)
         if older is not None:
             resid = resid - jnp.dot(jnp.transpose(summed[1]), older, precision=HI)
@@ -235,6 +242,7 @@
         alpha_list.append(summed[0])
         beta_list.append(jnp.transpose(lower))
         older = current
+        older_side = mean_side
         current = fresh
     next_block = jnp.transpose(current) * math.sqrt(width * gene_count)
     return (jnp.stack(alpha_list), jnp.stack(beta_list), next_block)

time: 312 us -> 307 us (0.984)
  waiting for transfers between devices: 112 us -> 85.5 us
  starting transfers between devices: 24.1 us -> 45.9 us
  matrix products: 20.2 us -> 16.5 us
  other arithmetic: 31.3 us -> 34.5 us
    ppermute x21 -> x27, starting transfers between devices: 12.2 us -> 36.2 us  [butterfly_sum(): x = x + lax.ppermute(x, axis, [(i, i ^ s) for i in range(n)])]
    ppermute x21 -> x27, waiting for transfers between devices: 74.8 us -> 58.3 us  [butterfly_sum(): x = x + lax.ppermute(x, axis, [(i, i ^ s) for i in range(n)])]
    ppermute x6 -> x4, waiting for transfers between devices: 12.2 us -> 2.47 us  [halving_sum(): other = lax.ppermute(x, axis, [(i, i ^ s) for i in range(n)])]
    ppermute x6 -> x4, waiting for transfers between devices: 24.8 us -> 16.5 us  [halving_sum(): x = keep + lax.ppermute(send, axis, [(i, i ^ s) for i in range(n)])]
    ppermute x0 -> x2, waiting for transfers between devices: none -> 8.23 us  [halving_sum(): x = x + lax.ppermute(x, axis, [(i, i ^ s) for i in range(n)])]
    ppermute x0 -> x2, starting transfers between devices: none -> 3.17 us  [halving_sum(): x = x + lax.ppermute(x, axis, [(i, i ^ s) for i in range(n)])]
  transfers between devices with their start and end apart: 33 -> 37, of which waited for: 28 -> 28; matrix products, arithmetic and copies ran while one was open for 5% -> 5% of each run, Pallas kernels for 10% -> 0%
where the time goes in v1:
time: 307 us; the launch traced here: 306 us
  Pallas kernels  115 us (37%)
  waiting for transfers between devices  85.5 us (28%)
  starting transfers between devices  45.9 us (15%)
  other arithmetic  34.5 us (11%)
  matrix products  16.5 us (5%)
  local copies, waits for them, and re-layouts  7.49 us (2%)
    pallas_call x2, Pallas kernels, forward(): pl.pallas_call(forward_kernel, grid=(rows // tr, width // tw), in_specs=i...  63.1 us
    ppermute x27, waiting for transfers between devices, butterfly_sum(): x = x + lax.ppermute(x, axis, [(i, i ^ s) for i in range(n)])  58.3 us
    pallas_call x2, Pallas kernels, backward(): pl.pallas_call(backward_kernel, grid=(width // tw, rows // tr), in_specs=...  52.1 us
    ppermute x27, starting transfers between devices, butterfly_sum(): x = x + lax.ppermute(x, axis, [(i, i ^ s) for i in range(n)])  36.2 us
    ppermute x4, waiting for transfers between devices, halving_sum(): x = keep + lax.ppermute(send, axis, [(i, i ^ s) for i in range(n)])  16.5 us
    another operation x5, other arithmetic, left_solve(): return lax.linalg.triangular_solve(lower, x, left_side=True, lower=True)  8.61 us
    ppermute x2, waiting for transfers between devices, halving_sum(): x = x + lax.ppermute(x, axis, [(i, i ^ s) for i in range(n)])  8.23 us
    another operation x6, other arithmetic, per_device(): lower = jnp.linalg.cholesky(g)  7.19 us
  transfers between devices with their start and end apart: 37, of which 28 were waited for; matrix products, arithmetic and copies ran while one was open for 5% of the time, Pallas kernels for 0%

profile of v1, /device:TPU:0, one launch (start us, length us, event | category | flops | bytes accessed | tf_op | source)
XLA Modules:
  0.0 306.2 jit_solution(4003122893408960737)
XLA Ops:
  6.2 32.4 %shard_map.58 = (f32[1536,32]{1,0:T(8,128)}, f32[1,8192]{1,0:T(1,128)}) custom-call(f32[1536,8192]{1,0:T(8,128)} %x_ref.7, f32[6,1,8192]{2,1,0:T(1,128)} %broadcast_in_dim_reshape.3.m_ref, bf16[96,8192]{1,0:T(8,128)(2,1)} %pad_maximum_fusion.s3_ref, bf16[64,8192]{1,0:T(8,128)(2,1)} %pad_maximum_fusion.2.s2_ref, bf16[32,8192]{1,0:T(8,128)(2,1)} %copy-done.3), custom_call_target="tpu_custom_call" | custom-call | tf_op jit(solution)/shard_map/pallas_call | solution.py:158
  39.6 3.1 %collective-permute-start = (f32[32,32]{0,1:T(8,128)S(1)}, f32[32,32]{0,1:T(8,128)S(1)}, u32[]{:S(2)}, u32[]{:S(2)}) collective-permute-start(f32[32,32]{0,1:T(8,128)S(1)} %fusion.65), channel_id=1, source_target_pairs={{0,1},{1,0},{2,3},{3,2},{4,5},{5,4},{6,7},{7,6},{8,9},{9,8},{10,11... | collective-permute-start | bytes 12296 | tf_op jit(solution)/shard_map/ppermute | solution.py:46
  44.4 3.0 collective-permute-start.1
  49.4 2.9 cholesky.59
  56.0 2.5 collective-permute-start.3
  59.2 2.4 custom-call.11
  61.7 4.1 %collective-permute-done.3 = f32[1536,32]{0,1:T(8,128)S(1)} collective-permute-done((f32[1536,32]{0,1:T(8,128)S(1)}, f32[1536,32]{0,1:T(8,128)S(1)}, u32[]{:S(2)}, u32[]{:S(2)}) %collective-permute-start.3) | collective-permute-done | bytes 196640 | tf_op jit(solution)/shard_map/ppermute | solution.py:46
  68.3 26.0 %shard_map.59 = f32[32,8192]{1,0:T(8,128)} custom-call(f32[1536,8192]{1,0:T(8,128)} %x_ref.7, f32[6,1,8192]{2,1,0:T(1,128)} %broadcast_in_dim_reshape.3.m_ref, bf16[96,1536]{1,0:T(8,128)(2,1)} %pad_maximum_fusion.4.s3_ref, bf16[64,1536]{1,0:T(8,128)(2,1)} %pad_maximum_fusion.6.s2_ref, bf16[32,1536]{1,0:T(8,128)(2,1)} %copy-done.6), custom_call_target="tpu_custom_call" | custom-call | tf_op jit(solution)/shard_map/pallas_call | solution.py:173
  100.1 6.9 %collective-permute-done.15 = f32[32,2048]{1,0:T(8,128)S(1)} collective-permute-done((f32[32,2048]{1,0:T(8,128)S(1)}, f32[32,2048]{1,0:T(8,128)S(1)}, u32[]{:S(2)}, u32[]{:S(2)}) %collective-permute-start.15) | collective-permute-done | bytes 262176 | tf_op jit(solution)/shard_map/ppermute | solution.py:64
  111.3 3.3 %collective-permute-done.16 = f32[32,2048]{1,0:T(8,128)S(1)} collective-permute-done((f32[32,2048]{1,0:T(8,128)S(1)}, f32[32,2048]{1,0:T(8,128)S(1)}, u32[]{:S(2)}, u32[]{:S(2)}) %collective-permute-start.16) | collective-permute-done | bytes 262176 | tf_op jit(solution)/shard_map/ppermute | solution.py:68
  118.9 2.5 collective-permute-done.17
  125.3 2.2 collective-permute-done.5
  129.1 2.2 collective-permute-done.6
  131.6 3.5 %collective-permute-done.7 = f32[1,32,32]{2,1,0:T(8,128)S(1)} collective-permute-done((f32[1,32,32]{2,1,0:T(8,128)S(1)}, f32[1,32,32]{2,1,0:T(8,128)S(1)}, u32[]{:S(2)}, u32[]{:S(2)}) %collective-permute-start.7) | collective-permute-done | bytes 4128 | tf_op jit(solution)/shard_map/ppermute | solution.py:46
  142.4 3.3 %collective-permute-done.13 = f32[32]{0:T(128)S(1)} collective-permute-done((f32[32]{0:T(128)S(1)}, f32[32]{0:T(128)S(1)}, u32[]{:S(2)}, u32[]{:S(2)}) %collective-permute-start.13) | collective-permute-done | bytes 160 | tf_op jit(solution)/shard_map/ppermute | solution.py:46
  152.9 3.5 %collective-permute-done.20 = f32[32,32]{0,1:T(8,128)S(1)} collective-permute-done((f32[32,32]{0,1:T(8,128)S(1)}, f32[32,32]{0,1:T(8,128)S(1)}, u32[]{:S(2)}, u32[]{:S(2)}) %collective-permute-start.20) | collective-permute-done | bytes 4128 | tf_op jit(solution)/shard_map/ppermute | solution.py:46
  156.4 2.9 cholesky.70
  160.7 2.4 custom-call.12
  166.9 30.7 %shard_map.60 = f32[1536,32]{1,0:T(8,128)} custom-call(f32[1536,8192]{1,0:T(8,128)} %x_ref.7, f32[6,1,8192]{2,1,0:T(1,128)} %broadcast_in_dim_reshape.3.m_ref, bf16[96,8192]{1,0:T(8,128)(2,1)} %pad_maximum_fusion.1.s3_ref, bf16[64,8192]{1,0:T(8,128)(2,1)} %pad_maximum_fusion.3.s2_ref, bf16[32,8192]{1,0:T(8,128)(2,1)} %copy-done.4), custom_call_target="tpu_custom_call" | custom-call | tf_op jit(solution)/shard_map/pallas_call | solution.py:158
  200.9 4.6 %collective-permute-done.21 = f32[1536,32]{0,1:T(8,128)S(1)} collective-permute-done((f32[1536,32]{0,1:T(8,128)S(1)}, f32[1536,32]{0,1:T(8,128)S(1)}, u32[]{:S(2)}, u32[]{:S(2)}) %collective-permute-start.21) | collective-permute-done | bytes 196640 | tf_op jit(solution)/shard_map/ppermute | solution.py:46
  205.9 8.3 %collective-permute-done.22 = f32[1536,32]{0,1:T(8,128)S(1)} collective-permute-done((f32[1536,32]{0,1:T(8,128)S(1)}, f32[1536,32]{0,1:T(8,128)S(1)}, u32[]{:S(2)}, u32[]{:S(2)}) %collective-permute-start.22) | collective-permute-done | bytes 196640 | tf_op jit(solution)/shard_map/ppermute | solution.py:46
  215.8 26.0 %shard_map.61 = f32[32,8192]{1,0:T(8,128)} custom-call(f32[1536,8192]{1,0:T(8,128)} %x_ref.7, f32[6,1,8192]{2,1,0:T(1,128)} %broadcast_in_dim_reshape.3.m_ref, bf16[96,1536]{1,0:T(8,128)(2,1)} %pad_maximum_fusion.5.s3_ref, bf16[64,1536]{1,0:T(8,128)(2,1)} %pad_maximum_fusion.7.s2_ref, bf16[32,1536]{1,0:T(8,128)(2,1)} %copy-done.7), custom_call_target="tpu_custom_call" | custom-call | tf_op jit(solution)/shard_map/pallas_call | solution.py:173
  248.6 5.9 %collective-permute-done.31 = f32[32,2048]{1,0:T(8,128)S(1)} collective-permute-done((f32[32,2048]{1,0:T(8,128)S(1)}, f32[32,2048]{1,0:T(8,128)S(1)}, u32[]{:S(2)}, u32[]{:S(2)}) %collective-permute-start.31) | collective-permute-done | bytes 262176 | tf_op jit(solution)/shard_map/ppermute | solution.py:64
  257.2 4.9 %collective-permute-done.32 = f32[32,2048]{1,0:T(8,128)S(1)} collective-permute-done((f32[32,2048]{1,0:T(8,128)S(1)}, f32[32,2048]{1,0:T(8,128)S(1)}, u32[]{:S(2)}, u32[]{:S(2)}) %collective-permute-start.32) | collective-permute-done | bytes 262176 | tf_op jit(solution)/shard_map/ppermute | solution.py:68
  264.3 5.2 %collective-permute-done.24 = f32[2,32,32]{2,1,0:T(8,128)S(1)} collective-permute-done((f32[2,32,32]{2,1,0:T(8,128)S(1)}, f32[2,32,32]{2,1,0:T(8,128)S(1)}, u32[]{:S(2)}, u32[]{:S(2)}) %collective-permute-start.24) | collective-permute-done | bytes 8224 | tf_op jit(solution)/shard_map/ppermute | solution.py:46
  271.1 2.4 collective-permute-done.25
  282.6 2.2 collective-permute-done.27
  288.6 3.5 %collective-permute-done.35 = f32[32,32]{0,1:T(8,128)S(1)} collective-permute-done((f32[32,32]{0,1:T(8,128)S(1)}, f32[32,32]{0,1:T(8,128)S(1)}, u32[]{:S(2)}, u32[]{:S(2)}) %collective-permute-start.35) | collective-permute-done | bytes 4128 | tf_op jit(solution)/shard_map/ppermute | solution.py:46
  293.9 2.8 collective-permute-done.36
  296.8 2.9 cholesky.81
  301.1 2.4 custom-call.13
  303.5 2.0 fusion
  (160 shorter events, 92.0 us)
Async XLA Ops:
  39.6 4.8 %collective-permute-start = (f32[32,32]{0,1:T(8,128)S(1)}, f32[32,32]{0,1:T(8,128)S(1)}, u32[]{:S(2)}, u32[]{:S(2)}) collective-permute-start(f32[32,32]{0,1:T(8,128)S(1)} %fusion.65), channel_id=1, source_target_pairs={{0,1},{1,0},{2,3},{3,2},{4,5},{5,4},{6,7},{7,6},{8,9},{9,8},{10,11... | collective-permute-start | bytes 12296 | tf_op jit(solution)/shard_map/ppermute | solution.py:46
  44.4 4.9 %collective-permute-start.1 = (f32[32,32]{0,1:T(8,128)S(1)}, f32[32,32]{0,1:T(8,128)S(1)}, u32[]{:S(2)}, u32[]{:S(2)}) collective-permute-start(f32[32,32]{0,1:T(8,128)S(1)} %add.136), channel_id=1, source_target_pairs={{0,2},{1,3},{2,0},{3,1},{4,6},{5,7},{6,4},{7,5},{8,10},{9,11},{10,... | collective-permute-start | bytes 12296 | tf_op jit(solution)/shard_map/ppermute | solution.py:46
  47.7 5.7 %collective-permute-start.2 = (f32[1536,32]{0,1:T(8,128)S(1)}, f32[1536,32]{0,1:T(8,128)S(1)}, u32[]{:S(2)}, u32[]{:S(2)}) collective-permute-start(f32[1536,32]{0,1:T(8,128)S(1)} %copy.21), channel_id=1, source_target_pairs={{0,1},{1,0},{2,3},{3,2},{4,5},{5,4},{6,7},{7,6},{8,9},{9,8},{10,11... | collective-permute-start | bytes 589832 | tf_op jit(solution)/shard_map/ppermute | solution.py:46
  56.0 9.7 %collective-permute-start.3 = (f32[1536,32]{0,1:T(8,128)S(1)}, f32[1536,32]{0,1:T(8,128)S(1)}, u32[]{:S(2)}, u32[]{:S(2)}) collective-permute-start(f32[1536,32]{0,1:T(8,128)S(1)} %copy.23), channel_id=1, source_target_pairs={{0,2},{1,3},{2,0},{3,1},{4,6},{5,7},{6,4},{7,5},{8,10},{9,11},{10,... | collective-permute-start | bytes 589832 | tf_op jit(solution)/shard_map/ppermute | solution.py:46
  98.6 8.4 %collective-permute-start.15 = (f32[32,2048]{1,0:T(8,128)S(1)}, f32[32,2048]{1,0:T(8,128)S(1)}, u32[]{:S(2)}, u32[]{:S(2)}) collective-permute-start(f32[32,2048]{1,0:T(8,128)S(1)} %constant_dynamic-slice_fusion.2), channel_id=1, source_target_pairs={{0,8},{4,12},{8,0},{12,4},{16,24},{20,28},{24,16},{28,20},{1,9},{5... | collective-permute-start | bytes 786440 | tf_op jit(solution)/shard_map/ppermute | solution.py:64
  107.0 7.6 %collective-permute-start.16 = (f32[32,2048]{1,0:T(8,128)S(1)}, f32[32,2048]{1,0:T(8,128)S(1)}, u32[]{:S(2)}, u32[]{:S(2)}) collective-permute-start(f32[32,2048]{1,0:T(8,128)S(1)} %dynamic-slice_add_fusion.3), channel_id=1, source_target_pairs={{0,16},{4,20},{8,24},{12,28},{16,0},{20,4},{24,8},{28,12},{1,17},{... | collective-permute-start | bytes 786440 | tf_op jit(solution)/shard_map/ppermute | solution.py:68
  109.9 7.4 %collective-permute-start.10 = (f32[8192]{0:T(1024)S(1)}, f32[8192]{0:T(1024)S(1)}, u32[]{:S(2)}, u32[]{:S(2)}) collective-permute-start(f32[8192]{0:T(1024)S(1)} %add.145), channel_id=1, source_target_pairs={{0,8},{4,12},{8,0},{12,4},{16,24},{20,28},{24,16},{28,20},{1,9},{5... | collective-permute-start | bytes 98312 | tf_op jit(solution)/shard_map/ppermute | solution.py:46
  114.7 6.7 %collective-permute-start.17 = (f32[32,2048]{1,0:T(8,128)S(1)}, f32[32,2048]{1,0:T(8,128)S(1)}, u32[]{:S(2)}, u32[]{:S(2)}) collective-permute-start(f32[32,2048]{1,0:T(8,128)S(1)} %add.158), channel_id=1, source_target_pairs={{0,8},{4,12},{8,0},{12,4},{16,24},{20,28},{24,16},{28,20},{1,9},{5... | collective-permute-start | bytes 786440 | tf_op jit(solution)/shard_map/ppermute | solution.py:71
  117.3 14.3 %collective-permute-start.11 = (f32[8192]{0:T(1024)S(1)}, f32[8192]{0:T(1024)S(1)}, u32[]{:S(2)}, u32[]{:S(2)}) collective-permute-start(f32[8192]{0:T(1024)S(1)} %add.146), channel_id=1, source_target_pairs={{0,16},{4,20},{8,24},{12,28},{16,0},{20,4},{24,8},{28,12},{1,17},{... | collective-permute-start | bytes 98312 | tf_op jit(solution)/shard_map/ppermute | solution.py:46
  121.4 24.3 %collective-permute-start.18 = (f32[32,4096]{1,0:T(8,128)S(1)}, f32[32,4096]{1,0:T(8,128)S(1)}, u32[]{:S(2)}, u32[]{:S(2)}) collective-permute-start(f32[32,4096]{1,0:T(8,128)S(1)} %maximum_select_fusion.2), channel_id=1, source_target_pairs={{0,4},{4,0},{8,12},{12,8},{16,20},{20,16},{24,28},{28,24},{1,5},{5... | collective-permute-start | bytes 1572872 | tf_op jit(solution)/shard_map/ppermute | solution.py:71
  123.8 3.7 %collective-permute-start.5 = (f32[1,32,32]{2,1,0:T(8,128)S(1)}, f32[1,32,32]{2,1,0:T(8,128)S(1)}, u32[]{:S(2)}, u32[]{:S(2)}) collective-permute-start(f32[1,32,32]{2,1,0:T(8,128)S(1)} %add.140), channel_id=1, source_target_pairs={{0,8},{4,12},{8,0},{12,4},{16,24},{20,28},{24,16},{28,20},{1,9},{5... | collective-permute-start | bytes 12296 | tf_op jit(solution)/shard_map/ppermute | solution.py:46
  127.6 3.7 %collective-permute-start.6 = (f32[1,32,32]{2,1,0:T(8,128)S(1)}, f32[1,32,32]{2,1,0:T(8,128)S(1)}, u32[]{:S(2)}, u32[]{:S(2)}) collective-permute-start(f32[1,32,32]{2,1,0:T(8,128)S(1)} %add.141), channel_id=1, source_target_pairs={{0,16},{4,20},{8,24},{12,28},{16,0},{20,4},{24,8},{28,12},{1,17},{... | collective-permute-start | bytes 12296 | tf_op jit(solution)/shard_map/ppermute | solution.py:46
  131.3 3.7 %collective-permute-start.7 = (f32[1,32,32]{2,1,0:T(8,128)S(1)}, f32[1,32,32]{2,1,0:T(8,128)S(1)}, u32[]{:S(2)}, u32[]{:S(2)}) collective-permute-start(f32[1,32,32]{2,1,0:T(8,128)S(1)} %add.142), channel_id=1, source_target_pairs={{0,1},{1,0},{2,3},{3,2},{4,5},{5,4},{6,7},{7,6},{8,9},{9,8},{10,11... | collective-permute-start | bytes 12296 | tf_op jit(solution)/shard_map/ppermute | solution.py:46
  135.0 10.7 %collective-permute-start.8 = (f32[1,32,32]{2,1,0:T(8,128)S(1)}, f32[1,32,32]{2,1,0:T(8,128)S(1)}, u32[]{:S(2)}, u32[]{:S(2)}) collective-permute-start(f32[1,32,32]{2,1,0:T(8,128)S(1)} %add.143), channel_id=1, source_target_pairs={{0,2},{1,3},{2,0},{3,1},{4,6},{5,7},{6,4},{7,5},{8,10},{9,11},{10,... | collective-permute-start | bytes 12296 | tf_op jit(solution)/shard_map/ppermute | solution.py:46
  141.3 4.4 %collective-permute-start.13 = (f32[32]{0:T(128)S(1)}, f32[32]{0:T(128)S(1)}, u32[]{:S(2)}, u32[]{:S(2)}) collective-permute-start(f32[32]{0:T(128)S(1)} %add.148), channel_id=1, source_target_pairs={{0,2},{1,3},{2,0},{3,1},{4,6},{5,7},{6,4},{7,5},{8,10},{9,11},{10,... | collective-permute-start | bytes 392 | tf_op jit(solution)/shard_map/ppermute | solution.py:46
  147.9 3.8 %collective-permute-start.19 = (f32[32,32]{0,1:T(8,128)S(1)}, f32[32,32]{0,1:T(8,128)S(1)}, u32[]{:S(2)}, u32[]{:S(2)}) collective-permute-start(f32[32,32]{0,1:T(8,128)S(1)} %fusion.66), channel_id=1, source_target_pairs={{0,1},{1,0},{2,3},{3,2},{4,5},{5,4},{6,7},{7,6},{8,9},{9,8},{10,11... | collective-permute-start | bytes 12296 | tf_op jit(solution)/shard_map/ppermute | solution.py:46
  151.7 4.6 %collective-permute-start.20 = (f32[32,32]{0,1:T(8,128)S(1)}, f32[32,32]{0,1:T(8,128)S(1)}, u32[]{:S(2)}, u32[]{:S(2)}) collective-permute-start(f32[32,32]{0,1:T(8,128)S(1)} %add.159), channel_id=1, source_target_pairs={{0,2},{1,3},{2,0},{3,1},{4,6},{5,7},{6,4},{7,5},{8,10},{9,11},{10,... | collective-permute-start | bytes 12296 | tf_op jit(solution)/shard_map/ppermute | solution.py:46
  198.9 6.5 %collective-permute-start.21 = (f32[1536,32]{0,1:T(8,128)S(1)}, f32[1536,32]{0,1:T(8,128)S(1)}, u32[]{:S(2)}, u32[]{:S(2)}) collective-permute-start(f32[1536,32]{0,1:T(8,128)S(1)} %copy.29), channel_id=1, source_target_pairs={{0,1},{1,0},{2,3},{3,2},{4,5},{5,4},{6,7},{7,6},{8,9},{9,8},{10,11... | collective-permute-start | bytes 589832 | tf_op jit(solution)/shard_map/ppermute | solution.py:46
  205.5 8.7 %collective-permute-start.22 = (f32[1536,32]{0,1:T(8,128)S(1)}, f32[1536,32]{0,1:T(8,128)S(1)}, u32[]{:S(2)}, u32[]{:S(2)}) collective-permute-start(f32[1536,32]{0,1:T(8,128)S(1)} %add.161), channel_id=1, source_target_pairs={{0,2},{1,3},{2,0},{3,1},{4,6},{5,7},{6,4},{7,5},{8,10},{9,11},{10,... | collective-permute-start | bytes 589832 | tf_op jit(solution)/shard_map/ppermute | solution.py:46
  246.1 8.4 %collective-permute-start.31 = (f32[32,2048]{1,0:T(8,128)S(1)}, f32[32,2048]{1,0:T(8,128)S(1)}, u32[]{:S(2)}, u32[]{:S(2)}) collective-permute-start(f32[32,2048]{1,0:T(8,128)S(1)} %constant_dynamic-slice_fusion), channel_id=1, source_target_pairs={{0,8},{4,12},{8,0},{12,4},{16,24},{20,28},{24,16},{28,20},{1,9},{5... | collective-permute-start | bytes 786440 | tf_op jit(solution)/shard_map/ppermute | solution.py:64
  254.5 7.6 %collective-permute-start.32 = (f32[32,2048]{1,0:T(8,128)S(1)}, f32[32,2048]{1,0:T(8,128)S(1)}, u32[]{:S(2)}, u32[]{:S(2)}) collective-permute-start(f32[32,2048]{1,0:T(8,128)S(1)} %dynamic-slice_add_fusion.2), channel_id=1, source_target_pairs={{0,16},{4,20},{8,24},{12,28},{16,0},{20,4},{24,8},{28,12},{1,17},{... | collective-permute-start | bytes 786440 | tf_op jit(solution)/shard_map/ppermute | solution.py:68
  257.1 6.6 %collective-permute-start.23 = (f32[2,32,32]{2,1,0:T(8,128)S(1)}, f32[2,32,32]{2,1,0:T(8,128)S(1)}, u32[]{:S(2)}, u32[]{:S(2)}) collective-permute-start(f32[2,32,32]{2,1,0:T(8,128)S(1)} %pad_maximum_fusion.8), channel_id=1, source_target_pairs={{0,4},{4,0},{8,12},{12,8},{16,20},{20,16},{24,28},{28,24},{1,5},{5... | collective-permute-start | bytes 24584 | tf_op jit(solution)/shard_map/ppermute | solution.py:46
  262.2 11.4 %collective-permute-start.33 = (f32[32,2048]{1,0:T(8,128)S(1)}, f32[32,2048]{1,0:T(8,128)S(1)}, u32[]{:S(2)}, u32[]{:S(2)}) collective-permute-start(f32[32,2048]{1,0:T(8,128)S(1)} %add.172), channel_id=1, source_target_pairs={{0,8},{4,12},{8,0},{12,4},{16,24},{20,28},{24,16},{28,20},{1,9},{5... | collective-permute-start | bytes 786440 | tf_op jit(solution)/shard_map/ppermute | solution.py:71
  263.7 5.8 %collective-permute-start.24 = (f32[2,32,32]{2,1,0:T(8,128)S(1)}, f32[2,32,32]{2,1,0:T(8,128)S(1)}, u32[]{:S(2)}, u32[]{:S(2)}) collective-permute-start(f32[2,32,32]{2,1,0:T(8,128)S(1)} %fusion.64), channel_id=1, source_target_pairs={{0,8},{4,12},{8,0},{12,4},{16,24},{20,28},{24,16},{28,20},{1,9},{5... | collective-permute-start | bytes 24584 | tf_op jit(solution)/shard_map/ppermute | solution.py:46
  269.5 4.0 %collective-permute-start.25 = (f32[2,32,32]{2,1,0:T(8,128)S(1)}, f32[2,32,32]{2,1,0:T(8,128)S(1)}, u32[]{:S(2)}, u32[]{:S(2)}) collective-permute-start(f32[2,32,32]{2,1,0:T(8,128)S(1)} %fusion.90), channel_id=1, source_target_pairs={{0,16},{4,20},{8,24},{12,28},{16,0},{20,4},{24,8},{28,12},{1,17},{... | collective-permute-start | bytes 24584 | tf_op jit(solution)/shard_map/ppermute | solution.py:46
  273.5 6.4 %collective-permute-start.26 = (f32[2,32,32]{2,1,0:T(8,128)S(1)}, f32[2,32,32]{2,1,0:T(8,128)S(1)}, u32[]{:S(2)}, u32[]{:S(2)}) collective-permute-start(f32[2,32,32]{2,1,0:T(8,128)S(1)} %add.165), channel_id=1, source_target_pairs={{0,1},{1,0},{2,3},{3,2},{4,5},{5,4},{6,7},{7,6},{8,9},{9,8},{10,11... | collective-permute-start | bytes 24584 | tf_op jit(solution)/shard_map/ppermute | solution.py:46
  273.6 12.4 %collective-permute-start.34 = (f32[32,4096]{1,0:T(8,128)S(1)}, f32[32,4096]{1,0:T(8,128)S(1)}, u32[]{:S(2)}, u32[]{:S(2)}) collective-permute-start(f32[32,4096]{1,0:T(8,128)S(1)} %maximum_select_fusion.3), channel_id=1, source_target_pairs={{0,4},{4,0},{8,12},{12,8},{16,20},{20,16},{24,28},{28,24},{1,5},{5... | collective-permute-start | bytes 1572872 | tf_op jit(solution)/shard_map/ppermute | solution.py:71
  274.6 3.6 %collective-permute-start.28 = (f32[32]{0:T(128)S(1)}, f32[32]{0:T(128)S(1)}, u32[]{:S(2)}, u32[]{:S(2)}) collective-permute-start(f32[32]{0:T(128)S(1)} %convolution_bitcast_fusion.3), channel_id=1, source_target_pairs={{0,1},{1,0},{2,3},{3,2},{4,5},{5,4},{6,7},{7,6},{8,9},{9,8},{10,11... | collective-permute-start | bytes 392 | tf_op jit(solution)/shard_map/ppermute | solution.py:46
  278.2 4.5 %collective-permute-start.29 = (f32[32]{0:T(128)S(1)}, f32[32]{0:T(128)S(1)}, u32[]{:S(2)}, u32[]{:S(2)}) collective-permute-start(f32[32]{0:T(128)S(1)} %add.168), channel_id=1, source_target_pairs={{0,2},{1,3},{2,0},{3,1},{4,6},{5,7},{6,4},{7,5},{8,10},{9,11},{10,... | collective-permute-start | bytes 392 | tf_op jit(solution)/shard_map/ppermute | solution.py:46
  280.0 4.9 %collective-permute-start.27 = (f32[2,32,32]{2,1,0:T(8,128)S(1)}, f32[2,32,32]{2,1,0:T(8,128)S(1)}, u32[]{:S(2)}, u32[]{:S(2)}) collective-permute-start(f32[2,32,32]{2,1,0:T(8,128)S(1)} %add.166), channel_id=1, source_target_pairs={{0,2},{1,3},{2,0},{3,1},{4,6},{5,7},{6,4},{7,5},{8,10},{9,11},{10,... | collective-permute-start | bytes 24584 | tf_op jit(solution)/shard_map/ppermute | solution.py:46
  288.3 3.8 %collective-permute-start.35 = (f32[32,32]{0,1:T(8,128)S(1)}, f32[32,32]{0,1:T(8,128)S(1)}, u32[]{:S(2)}, u32[]{:S(2)}) collective-permute-start(f32[32,32]{0,1:T(8,128)S(1)} %fusion.67), channel_id=1, source_target_pairs={{0,1},{1,0},{2,3},{3,2},{4,5},{5,4},{6,7},{7,6},{8,9},{9,8},{10,11... | collective-permute-start | bytes 12296 | tf_op jit(solution)/shard_map/ppermute | solution.py:46
  292.1 4.6 %collective-permute-start.36 = (f32[32,32]{0,1:T(8,128)S(1)}, f32[32,32]{0,1:T(8,128)S(1)}, u32[]{:S(2)}, u32[]{:S(2)}) collective-permute-start(f32[32,32]{0,1:T(8,128)S(1)} %add.173), channel_id=1, source_target_pairs={{0,2},{1,3},{2,0},{3,1},{4,6},{5,7},{6,4},{7,5},{8,10},{9,11},{10,... | collective-permute-start | bytes 12296 | tf_op jit(solution)/shard_map/ppermute | solution.py:46
  (14 other events, 92.2 us)

commit v2 on v1

--- a/solution.py
+++ b/solution.py
@@ -73,6 +73,60 @@
         hi_first = jnp.concatenate([other, x], axis=dim)
         x = jnp.where(bit == 0, lo_first, hi_first)
     return x
+
+
+def pack_rows(x, extra):
+    w = x.shape[1]
+    flat = extra.reshape(-1)
+    rows = -(-flat.shape[0] // w)
+    flat = jnp.pad(flat, (0, rows * w - flat.shape[0]))
+    return jnp.concatenate([x, flat.reshape(rows, w)], axis=0)
+
+
+def unpack_rows(x, r, extra_shape):
+    size = math.prod(extra_shape)
+    return x[:r], x[r:].reshape(-1)[:size].reshape(extra_shape)
+
+
+def gene_sum_with(x, extra):
+    r = x.shape[0]
+    return unpack_rows(butterfly_sum(pack_rows(x, extra), "gene"), r, extra.shape)
+
+
+def cell_image_sum(part, extra):
+    axis = "cell"
+    n = lax.axis_size(axis)
+    if n & (n - 1) or part.shape[1] % n:
+        return lax.psum(part, axis), lax.psum(extra, axis)
+    me = lax.axis_index(axis)
+    levels = max(n.bit_length() - 2, 0)
+    k = part.shape[0]
+    x = part
+    s = 1
+    bits = []
+    for _ in range(levels):
+        half = x.shape[1] // 2
+        bit = (me // s) % 2
+        keep = lax.dynamic_slice_in_dim(x, bit * half, half, axis=1)
+        send = lax.dynamic_slice_in_dim(x, (1 - bit) * half, half, axis=1)
+        got = lax.ppermute(pack_rows(send, extra), axis, [(i, i ^ s) for i in range(n)])
+        got_x, got_e = unpack_rows(got, k, extra.shape)
+        x = keep + got_x
+        extra = extra + got_e
+        bits.append((s, bit))
+        s *= 2
+    while s < n:
+        got = lax.ppermute(pack_rows(x, extra), axis, [(i, i ^ s) for i in range(n)])
+        got_x, got_e = unpack_rows(got, k, extra.shape)
+        x = x + got_x
+        extra = extra + got_e
+        s *= 2
+    for s, bit in reversed(bits):
+        other = lax.ppermute(x, axis, [(i, i ^ s) for i in range(n)])
+        lo_first = jnp.concatenate([x, other], axis=1)
+        hi_first = jnp.concatenate([other, x], axis=1)
+        x = jnp.where(bit == 0, lo_first, hi_first)
+    return x, extra
 
 
 def _nt(a, b):
@@ -211,11 +265,15 @@
 
     y_start, colsum = forward(expression, mexp, start_t, True)
     start_t = lax.optimization_barrier((start_t, y_start))[0]
-    gram0 = butterfly_sum(row_gram(start_t, start_t), "gene")
+    extra = jnp.concatenate([row_gram(start_t, start_t), jnp.sum(y_start, axis=0)[None, :]], axis=0)
+    y_start, extra = gene_sum_with(y_start, extra)
+    gram0 = extra[:-1]
     lower0 = jnp.linalg.cholesky(gram0)
     current = left_solve(lower0, start_t)
-    means = butterfly_sum(colsum[0], "cell") / cells
-    y = right_solve(lower0, butterfly_sum(y_start, "gene"))
+    y = right_solve(lower0, y_start)
+    totals = butterfly_sum(jnp.concatenate([colsum[0], extra[-1]]), "cell")
+    means = totals[:width] / cells
+    mean_side = right_solve(lower0, (totals[width:] / cells)[None, :])[0]
 
     older = None
     older_side = None
@@ -223,14 +281,14 @@
     beta_list = []
     for step in range(STEPS):
         if step > 0:
-            y = butterfly_sum(forward(expression, mexp, current, False)[0], "gene")
-        mean_side = butterfly_sum(jnp.dot(current, means, precision=HI), "gene")
+            y, mean_side = gene_sum_with(forward(expression, mexp, current, False)[0],
+                                         jnp.dot(current, means, precision=HI))
         part = backward(expression, mexp, y)
         basis = [current] if older is None else [current, older]
         sides = [mean_side] if older is None else [mean_side, older_side]
         proj_part = jnp.stack([row_gram(v, part) for v in basis])
-        proj_raw = butterfly_sum(butterfly_sum(proj_part, "cell"), "gene")
-        raw = halving_sum(part, "cell", 1)
+        raw, proj_cell = cell_image_sum(part, proj_part)
+        proj_raw = butterfly_sum(proj_cell, "gene")
         image = raw / cells - mean_side[:, None] * means[None, :]
         summed = [proj_raw[t] / cells - sides[t][:, None] * mean_side[None, :] for t in range(len(basis))]
         resid = image - jnp.dot(jnp.transpose(summed[0]), current, precision=HI)

time: 307 us -> 308 us (level)
  starting transfers between devices: 45.9 us -> 27.3 us
  waiting for transfers between devices: 85.5 us -> 99.6 us
  other arithmetic: 34.5 us -> 37.7 us
    ppermute x27 -> x15, starting transfers between devices: 36.2 us -> 18.1 us  [butterfly_sum(): x = x + lax.ppermute(x, axis, [(i, i ^ s) for i in range(n)])]
    ppermute x10, waiting for transfers between devices: 27.2 us -> 40.5 us  [the longest x4 21.2 us: cell_image_sum(): lax.ppermute(pack_rows(send, extra), axis, [(i, i ^ s) for i in range(n)])]
    ppermute x27 -> x15, waiting for transfers between devices: 58.3 us -> 59.1 us  [butterfly_sum(): x = x + lax.ppermute(x, axis, [(i, i ^ s) for i in range(n)])]
  transfers between devices with their start and end apart: 37 -> 25, of which waited for: 28 -> 20; matrix products, arithmetic and copies ran while one was open for 5% -> 1% of each run, Pallas kernels for 0% -> 0%
where the time goes in v2:
time: 308 us
  Pallas kernels  115 us (37%)
  waiting for transfers between devices  99.6 us (32%)
  other arithmetic  37.7 us (12%)
  starting transfers between devices  27.3 us (9%)
  matrix products  17.9 us (6%)
  local copies, waits for them, and re-layouts  8.94 us (3%)
    pallas_call x2, Pallas kernels, forward(): pl.pallas_call(forward_kernel, grid=(rows // tr, width // tw), in_specs=i...  63 us
    ppermute x15, waiting for transfers between devices, butterfly_sum(): x = x + lax.ppermute(x, axis, [(i, i ^ s) for i in range(n)])  59.1 us
    pallas_call x2, Pallas kernels, backward(): pl.pallas_call(backward_kernel, grid=(width // tw, rows // tr), in_specs=...  52.1 us
    ppermute x4, waiting for transfers between devices, cell_image_sum(): lax.ppermute(pack_rows(send, extra), axis, [(i, i ^ s) for i in range(n)])  21.2 us
    ppermute x15, starting transfers between devices, butterfly_sum(): x = x + lax.ppermute(x, axis, [(i, i ^ s) for i in range(n)])  18.1 us
    ppermute x2, waiting for transfers between devices, cell_image_sum(): lax.ppermute(pack_rows(x, extra), axis, [(i, i ^ s) for i in range(n)])  14.5 us
    another operation x5, other arithmetic, left_solve(): return lax.linalg.triangular_solve(lower, x, left_side=True, lower=True)  8.61 us
    dot_general x6, matrix products, row_gram(): lax.dot_general(a, b, (((1,), (1,)), ((), ())), precision=HI, preferred_e...  8.31 us
  transfers between devices with their start and end apart: 25, of which 20 were waited for; matrix products, arithmetic and copies ran while one was open for 1% of the time, Pallas kernels for 0%

profile of v2, /device:TPU:0, one launch (start us, length us, event | category | flops | bytes accessed | tf_op | source)
XLA Modules:
  0.0 307.7 jit_solution(9516220255857954867)
XLA Ops:
  6.2 32.3 %shard_map.58 = (f32[1536,32]{1,0:T(8,128)}, f32[1,8192]{1,0:T(1,128)}) custom-call(f32[1536,8192]{1,0:T(8,128)} %x_ref.7, f32[6,1,8192]{2,1,0:T(1,128)} %broadcast_in_dim_reshape.2.m_ref, bf16[96,8192]{1,0:T(8,128)(2,1)} %pad_maximum_fusion.s3_ref, bf16[64,8192]{1,0:T(8,128)(2,1)} %pad_maximum_fusion.2.s2_ref, bf16[32,8192]{1,0:T(8,128)(2,1)} %copy-done.3), custom_call_target="tpu_custom_call" | custom-call | tf_op jit(solution)/shard_map/pallas_call | solution.py:212
  42.5 3.0 collective-permute-start
  45.5 5.2 %collective-permute-done = f32[1569,32]{0,1:T(8,128)S(1)} collective-permute-done((f32[1569,32]{0,1:T(8,128)S(1)}, f32[1569,32]{0,1:T(8,128)S(1)}, u32[]{:S(2)}, u32[]{:S(2)}) %collective-permute-start) | collective-permute-done | bytes 200864 | tf_op jit(solution)/shard_map/ppermute | solution.py:46
  50.8 2.8 collective-permute-start.1
  53.6 9.1 %collective-permute-done.1 = f32[1569,32]{0,1:T(8,128)S(1)} collective-permute-done((f32[1569,32]{0,1:T(8,128)S(1)}, f32[1569,32]{0,1:T(8,128)S(1)}, u32[]{:S(2)}, u32[]{:S(2)}) %collective-permute-start.1) | collective-permute-done | bytes 200864 | tf_op jit(solution)/shard_map/ppermute | solution.py:46
  62.9 2.9 cholesky.59
  67.1 2.4 custom-call.13
  72.5 26.0 %shard_map.59 = f32[32,8192]{1,0:T(8,128)} custom-call(f32[1536,8192]{1,0:T(8,128)} %x_ref.7, f32[6,1,8192]{2,1,0:T(1,128)} %broadcast_in_dim_reshape.2.m_ref, bf16[96,1536]{1,0:T(8,128)(2,1)} %pad_maximum_fusion.10.s3_ref, bf16[64,1536]{1,0:T(8,128)(2,1)} %pad_maximum_fusion.13.s2_ref, bf16[32,1536]{1,0:T(8,128)(2,1)} %copy-done.5), custom_call_target="tpu_custom_call" | custom-call | tf_op jit(solution)/shard_map/pallas_call | solution.py:227
  107.9 8.4 %collective-permute-done.3 = f32[33,2048]{1,0:T(8,128)S(1)} collective-permute-done((f32[33,2048]{1,0:T(8,128)S(1)}, f32[33,2048]{1,0:T(8,128)S(1)}, u32[]{:S(2)}, u32[]{:S(2)}) %collective-permute-start.3) | collective-permute-done | bytes 270368 | tf_op jit(solution)/shard_map/ppermute | solution.py:112
  118.2 7.3 %collective-permute-done.4 = f32[33,2048]{1,0:T(8,128)S(1)} collective-permute-done((f32[33,2048]{1,0:T(8,128)S(1)}, f32[33,2048]{1,0:T(8,128)S(1)}, u32[]{:S(2)}, u32[]{:S(2)}) %collective-permute-start.4) | collective-permute-done | bytes 270368 | tf_op jit(solution)/shard_map/ppermute | solution.py:119
  127.7 5.3 %collective-permute-done.8 = f32[8224]{0:T(1024)S(1)} collective-permute-done((f32[8224]{0:T(1024)S(1)}, f32[8224]{0:T(1024)S(1)}, u32[]{:S(2)}, u32[]{:S(2)}) %collective-permute-start.8) | collective-permute-done | bytes 32928 | tf_op jit(solution)/shard_map/ppermute | solution.py:46
  134.4 2.6 collective-permute-done.9
  137.8 3.2 %collective-permute-done.5 = f32[1,32,32]{2,1,0:T(8,128)S(1)} collective-permute-done((f32[1,32,32]{2,1,0:T(8,128)S(1)}, f32[1,32,32]{2,1,0:T(8,128)S(1)}, u32[]{:S(2)}, u32[]{:S(2)}) %collective-permute-start.5) | collective-permute-done | bytes 4128 | tf_op jit(solution)/shard_map/ppermute | solution.py:46
  143.0 2.6 collective-permute-done.6
  148.9 2.8 collective-permute-done.12
  153.7 2.6 collective-permute-done.13
  156.4 2.9 cholesky.70
  160.7 2.4 custom-call.14
  166.8 30.7 %shard_map.60 = f32[1536,32]{1,0:T(8,128)} custom-call(f32[1536,8192]{1,0:T(8,128)} %x_ref.7, f32[6,1,8192]{2,1,0:T(1,128)} %broadcast_in_dim_reshape.2.m_ref, bf16[96,8192]{1,0:T(8,128)(2,1)} %pad_maximum_fusion.1.s3_ref, bf16[64,8192]{1,0:T(8,128)(2,1)} %pad_maximum_fusion.3.s2_ref, bf16[32,8192]{1,0:T(8,128)(2,1)} %copy-done.4), custom_call_target="tpu_custom_call" | custom-call | tf_op jit(solution)/shard_map/pallas_call | solution.py:212
  200.9 7.1 %collective-permute-done.14 = f32[1537,32]{0,1:T(8,128)S(1)} collective-permute-done((f32[1537,32]{0,1:T(8,128)S(1)}, f32[1537,32]{0,1:T(8,128)S(1)}, u32[]{:S(2)}, u32[]{:S(2)}) %collective-permute-start.14) | collective-permute-done | bytes 196768 | tf_op jit(solution)/shard_map/ppermute | solution.py:46
  210.1 6.7 %collective-permute-done.15 = f32[1537,32]{0,1:T(8,128)S(1)} collective-permute-done((f32[1537,32]{0,1:T(8,128)S(1)}, f32[1537,32]{0,1:T(8,128)S(1)}, u32[]{:S(2)}, u32[]{:S(2)}) %collective-permute-start.15) | collective-permute-done | bytes 196768 | tf_op jit(solution)/shard_map/ppermute | solution.py:46
  218.3 26.0 %shard_map.61 = f32[32,8192]{1,0:T(8,128)} custom-call(f32[1536,8192]{1,0:T(8,128)} %x_ref.7, f32[6,1,8192]{2,1,0:T(1,128)} %broadcast_in_dim_reshape.2.m_ref, bf16[96,1536]{1,0:T(8,128)(2,1)} %pad_maximum_fusion.11.s3_ref, bf16[64,1536]{1,0:T(8,128)(2,1)} %pad_maximum_fusion.14.s2_ref, bf16[32,1536]{1,0:T(8,128)(2,1)} %copy-done.6), custom_call_target="tpu_custom_call" | custom-call | tf_op jit(solution)/shard_map/pallas_call | solution.py:227
  244.4 2.3 convolution_bitcast_fusion
  250.6 2.4 collective-permute-done.16
  256.6 8.2 %collective-permute-done.17 = f32[33,2048]{1,0:T(8,128)S(1)} collective-permute-done((f32[33,2048]{1,0:T(8,128)S(1)}, f32[33,2048]{1,0:T(8,128)S(1)}, u32[]{:S(2)}, u32[]{:S(2)}) %collective-permute-start.17) | collective-permute-done | bytes 270368 | tf_op jit(solution)/shard_map/ppermute | solution.py:112
  266.6 7.3 %collective-permute-done.18 = f32[33,2048]{1,0:T(8,128)S(1)} collective-permute-done((f32[33,2048]{1,0:T(8,128)S(1)}, f32[33,2048]{1,0:T(8,128)S(1)}, u32[]{:S(2)}, u32[]{:S(2)}) %collective-permute-start.18) | collective-permute-done | bytes 270368 | tf_op jit(solution)/shard_map/ppermute | solution.py:119
  275.8 4.8 %collective-permute-done.21 = f32[32,2048]{1,0:T(8,128)S(1)} collective-permute-done((f32[32,2048]{1,0:T(8,128)S(1)}, f32[32,2048]{1,0:T(8,128)S(1)}, u32[]{:S(2)}, u32[]{:S(2)}) %collective-permute-start.21) | collective-permute-done | bytes 262176 | tf_op jit(solution)/shard_map/ppermute | solution.py:125
  281.2 5.1 %collective-permute-done.20 = f32[2,32,32]{2,1,0:T(8,128)S(1)} collective-permute-done((f32[2,32,32]{2,1,0:T(8,128)S(1)}, f32[2,32,32]{2,1,0:T(8,128)S(1)}, u32[]{:S(2)}, u32[]{:S(2)}) %collective-permute-start.20) | collective-permute-done | bytes 8224 | tf_op jit(solution)/shard_map/ppermute | solution.py:46
  290.0 3.5 %collective-permute-done.23 = f32[32,32]{0,1:T(8,128)S(1)} collective-permute-done((f32[32,32]{0,1:T(8,128)S(1)}, f32[32,32]{0,1:T(8,128)S(1)}, u32[]{:S(2)}, u32[]{:S(2)}) %collective-permute-start.23) | collective-permute-done | bytes 4128 | tf_op jit(solution)/shard_map/ppermute | solution.py:46
  295.0 3.2 %collective-permute-done.24 = f32[32,32]{0,1:T(8,128)S(1)} collective-permute-done((f32[32,32]{0,1:T(8,128)S(1)}, f32[32,32]{0,1:T(8,128)S(1)}, u32[]{:S(2)}, u32[]{:S(2)}) %collective-permute-start.24) | collective-permute-done | bytes 4128 | tf_op jit(solution)/shard_map/ppermute | solution.py:46
  298.2 2.9 cholesky.81
  302.5 2.4 custom-call.15
  (161 shorter events, 69.8 us)
Async XLA Ops:
  3.9 2.4 copy-start.3
  38.5 2.9 copy-start
  42.5 8.3 %collective-permute-start = (f32[1569,32]{0,1:T(8,128)S(1)}, f32[1569,32]{0,1:T(8,128)S(1)}, u32[]{:S(2)}, u32[]{:S(2)}) collective-permute-start(f32[1569,32]{0,1:T(8,128)S(1)} %concatenate.79), channel_id=1, source_target_pairs={{0,1},{1,0},{2,3},{3,2},{4,5},{5,4},{6,7},{7,6},{8,9},{9,8},{10,11... | collective-permute-start | bytes 602504 | tf_op jit(solution)/shard_map/ppermute | solution.py:46
  50.8 12.0 %collective-permute-start.1 = (f32[1569,32]{0,1:T(8,128)S(1)}, f32[1569,32]{0,1:T(8,128)S(1)}, u32[]{:S(2)}, u32[]{:S(2)}) collective-permute-start(f32[1569,32]{0,1:T(8,128)S(1)} %add.140), channel_id=1, source_target_pairs={{0,2},{1,3},{2,0},{3,1},{4,6},{5,7},{6,4},{7,5},{8,10},{9,11},{10,... | collective-permute-start | bytes 602504 | tf_op jit(solution)/shard_map/ppermute | solution.py:46
  70.0 2.5 copy-start.5
  98.5 6.8 %copy-start.2 = (f32[32,8192]{1,0:T(8,128)S(1)}, f32[32,8192]{1,0:T(8,128)}, u32[]{:S(2)}) copy-start(f32[32,8192]{1,0:T(8,128)} %shard_map.59) | copy-start | bytes 3145732
  102.0 2.3 collective-permute-start.2
  105.3 12.9 %copy-start.7 = (f32[1,8192]{1,0:T(1,128)S(1)}, f32[1,8192]{1,0:T(1,128)}, u32[]{:S(2)}) copy-start(f32[1,8192]{1,0:T(1,128)} %get-tuple-element.10) | copy-start | bytes 98308
  106.4 9.8 %collective-permute-start.3 = (f32[33,2048]{1,0:T(8,128)S(1)}, f32[33,2048]{1,0:T(8,128)S(1)}, u32[]{:S(2)}, u32[]{:S(2)}) collective-permute-start(f32[33,2048]{1,0:T(8,128)S(1)} %pad_maximum_fusion.6), channel_id=1, source_target_pairs={{0,8},{4,12},{8,0},{12,4},{16,24},{20,28},{24,16},{28,20},{1,9},{5... | collective-permute-start | bytes 811016 | tf_op jit(solution)/shard_map/ppermute | solution.py:112
  116.5 9.0 %collective-permute-start.4 = (f32[33,2048]{1,0:T(8,128)S(1)}, f32[33,2048]{1,0:T(8,128)S(1)}, u32[]{:S(2)}, u32[]{:S(2)}) collective-permute-start(f32[33,2048]{1,0:T(8,128)S(1)} %pad_maximum_fusion.7), channel_id=1, source_target_pairs={{0,16},{4,20},{8,24},{12,28},{16,0},{20,4},{24,8},{28,12},{1,17},{... | collective-permute-start | bytes 811016 | tf_op jit(solution)/shard_map/ppermute | solution.py:119
  118.2 8.8 %collective-permute-start.7 = (f32[8224]{0:T(1024)S(1)}, f32[8224]{0:T(1024)S(1)}, u32[]{:S(2)}, u32[]{:S(2)}) collective-permute-start(f32[8224]{0:T(1024)S(1)} %pad_maximum_fusion.15), channel_id=1, source_target_pairs={{0,4},{4,0},{8,12},{12,8},{16,20},{20,16},{24,28},{28,24},{1,5},{5... | collective-permute-start | bytes 98696 | tf_op jit(solution)/shard_map/ppermute | solution.py:46
  125.5 11.5 %collective-permute-start.10 = (f32[32,2048]{1,0:T(8,128)S(1)}, f32[32,2048]{1,0:T(8,128)S(1)}, u32[]{:S(2)}, u32[]{:S(2)}) collective-permute-start(f32[32,2048]{1,0:T(8,128)S(1)} %slice_add_fusion.4), channel_id=1, source_target_pairs={{0,8},{4,12},{8,0},{12,4},{16,24},{20,28},{24,16},{28,20},{1,9},{5... | collective-permute-start | bytes 786440 | tf_op jit(solution)/shard_map/ppermute | solution.py:125
  127.0 6.0 %collective-permute-start.8 = (f32[8224]{0:T(1024)S(1)}, f32[8224]{0:T(1024)S(1)}, u32[]{:S(2)}, u32[]{:S(2)}) collective-permute-start(f32[8224]{0:T(1024)S(1)} %fusion.65), channel_id=1, source_target_pairs={{0,8},{4,12},{8,0},{12,4},{16,24},{20,28},{24,16},{28,20},{1,9},{5... | collective-permute-start | bytes 98696 | tf_op jit(solution)/shard_map/ppermute | solution.py:46
  133.0 4.0 %collective-permute-start.9 = (f32[8224]{0:T(1024)S(1)}, f32[8224]{0:T(1024)S(1)}, u32[]{:S(2)}, u32[]{:S(2)}) collective-permute-start(f32[8224]{0:T(1024)S(1)} %add.157), channel_id=1, source_target_pairs={{0,16},{4,20},{8,24},{12,28},{16,0},{20,4},{24,8},{28,12},{1,17},{... | collective-permute-start | bytes 98696 | tf_op jit(solution)/shard_map/ppermute | solution.py:46
  137.1 8.5 %collective-permute-start.11 = (f32[32,4096]{1,0:T(8,128)S(1)}, f32[32,4096]{1,0:T(8,128)S(1)}, u32[]{:S(2)}, u32[]{:S(2)}) collective-permute-start(f32[32,4096]{1,0:T(8,128)S(1)} %maximum_select_fusion.2), channel_id=1, source_target_pairs={{0,4},{4,0},{8,12},{12,8},{16,20},{20,16},{24,28},{28,24},{1,5},{5... | collective-permute-start | bytes 1572872 | tf_op jit(solution)/shard_map/ppermute | solution.py:125
  137.2 3.8 %collective-permute-start.5 = (f32[1,32,32]{2,1,0:T(8,128)S(1)}, f32[1,32,32]{2,1,0:T(8,128)S(1)}, u32[]{:S(2)}, u32[]{:S(2)}) collective-permute-start(f32[1,32,32]{2,1,0:T(8,128)S(1)} %add_bitcast_fusion), channel_id=1, source_target_pairs={{0,1},{1,0},{2,3},{3,2},{4,5},{5,4},{6,7},{7,6},{8,9},{9,8},{10,11... | collective-permute-start | bytes 12296 | tf_op jit(solution)/shard_map/ppermute | solution.py:46
  141.0 4.6 %collective-permute-start.6 = (f32[1,32,32]{2,1,0:T(8,128)S(1)}, f32[1,32,32]{2,1,0:T(8,128)S(1)}, u32[]{:S(2)}, u32[]{:S(2)}) collective-permute-start(f32[1,32,32]{2,1,0:T(8,128)S(1)} %add.154), channel_id=1, source_target_pairs={{0,2},{1,3},{2,0},{3,1},{4,6},{5,7},{6,4},{7,5},{8,10},{9,11},{10,... | collective-permute-start | bytes 12296 | tf_op jit(solution)/shard_map/ppermute | solution.py:46
  147.9 3.8 %collective-permute-start.12 = (f32[32,32]{0,1:T(8,128)S(1)}, f32[32,32]{0,1:T(8,128)S(1)}, u32[]{:S(2)}, u32[]{:S(2)}) collective-permute-start(f32[32,32]{0,1:T(8,128)S(1)} %fusion.69), channel_id=1, source_target_pairs={{0,1},{1,0},{2,3},{3,2},{4,5},{5,4},{6,7},{7,6},{8,9},{9,8},{10,11... | collective-permute-start | bytes 12296 | tf_op jit(solution)/shard_map/ppermute | solution.py:46
  151.7 4.6 %collective-permute-start.13 = (f32[32,32]{0,1:T(8,128)S(1)}, f32[32,32]{0,1:T(8,128)S(1)}, u32[]{:S(2)}, u32[]{:S(2)}) collective-permute-start(f32[32,32]{0,1:T(8,128)S(1)} %add.160), channel_id=1, source_target_pairs={{0,2},{1,3},{2,0},{3,1},{4,6},{5,7},{6,4},{7,5},{8,10},{9,11},{10,... | collective-permute-start | bytes 12296 | tf_op jit(solution)/shard_map/ppermute | solution.py:46
  199.9 8.2 %collective-permute-start.14 = (f32[1537,32]{0,1:T(8,128)S(1)}, f32[1537,32]{0,1:T(8,128)S(1)}, u32[]{:S(2)}, u32[]{:S(2)}) collective-permute-start(f32[1537,32]{0,1:T(8,128)S(1)} %pad_maximum_fusion.12), channel_id=1, source_target_pairs={{0,1},{1,0},{2,3},{3,2},{4,5},{5,4},{6,7},{7,6},{8,9},{9,8},{10,11... | collective-permute-start | bytes 590216 | tf_op jit(solution)/shard_map/ppermute | solution.py:46
  208.1 8.7 %collective-permute-start.15 = (f32[1537,32]{0,1:T(8,128)S(1)}, f32[1537,32]{0,1:T(8,128)S(1)}, u32[]{:S(2)}, u32[]{:S(2)}) collective-permute-start(f32[1537,32]{0,1:T(8,128)S(1)} %fusion.66), channel_id=1, source_target_pairs={{0,2},{1,3},{2,0},{3,1},{4,6},{5,7},{6,4},{7,5},{8,10},{9,11},{10,... | collective-permute-start | bytes 590216 | tf_op jit(solution)/shard_map/ppermute | solution.py:46
  216.9 1.4 copy-start.6
  244.4 2.3 copy-start.1
  250.5 2.4 collective-permute-start.16
  255.0 9.8 %collective-permute-start.17 = (f32[33,2048]{1,0:T(8,128)S(1)}, f32[33,2048]{1,0:T(8,128)S(1)}, u32[]{:S(2)}, u32[]{:S(2)}) collective-permute-start(f32[33,2048]{1,0:T(8,128)S(1)} %pad_maximum_fusion.8), channel_id=1, source_target_pairs={{0,8},{4,12},{8,0},{12,4},{16,24},{20,28},{24,16},{28,20},{1,9},{5... | collective-permute-start | bytes 811016 | tf_op jit(solution)/shard_map/ppermute | solution.py:112
  264.9 9.0 %collective-permute-start.18 = (f32[33,2048]{1,0:T(8,128)S(1)}, f32[33,2048]{1,0:T(8,128)S(1)}, u32[]{:S(2)}, u32[]{:S(2)}) collective-permute-start(f32[33,2048]{1,0:T(8,128)S(1)} %pad_maximum_fusion.9), channel_id=1, source_target_pairs={{0,16},{4,20},{8,24},{12,28},{16,0},{20,4},{24,8},{28,12},{1,17},{... | collective-permute-start | bytes 811016 | tf_op jit(solution)/shard_map/ppermute | solution.py:119
  273.9 6.7 %collective-permute-start.21 = (f32[32,2048]{1,0:T(8,128)S(1)}, f32[32,2048]{1,0:T(8,128)S(1)}, u32[]{:S(2)}, u32[]{:S(2)}) collective-permute-start(f32[32,2048]{1,0:T(8,128)S(1)} %slice_add_fusion.2), channel_id=1, source_target_pairs={{0,8},{4,12},{8,0},{12,4},{16,24},{20,28},{24,16},{28,20},{1,9},{5... | collective-permute-start | bytes 786440 | tf_op jit(solution)/shard_map/ppermute | solution.py:125
  275.6 5.2 %collective-permute-start.19 = (f32[2,32,32]{2,1,0:T(8,128)S(1)}, f32[2,32,32]{2,1,0:T(8,128)S(1)}, u32[]{:S(2)}, u32[]{:S(2)}) collective-permute-start(f32[2,32,32]{2,1,0:T(8,128)S(1)} %add_add_fusion), channel_id=1, source_target_pairs={{0,1},{1,0},{2,3},{3,2},{4,5},{5,4},{6,7},{7,6},{8,9},{9,8},{10,11... | collective-permute-start | bytes 24584 | tf_op jit(solution)/shard_map/ppermute | solution.py:46
  280.6 6.7 %collective-permute-start.22 = (f32[32,4096]{1,0:T(8,128)S(1)}, f32[32,4096]{1,0:T(8,128)S(1)}, u32[]{:S(2)}, u32[]{:S(2)}) collective-permute-start(f32[32,4096]{1,0:T(8,128)S(1)} %maximum_select_fusion.3), channel_id=1, source_target_pairs={{0,4},{4,0},{8,12},{12,8},{16,20},{20,16},{24,28},{28,24},{1,5},{5... | collective-permute-start | bytes 1572872 | tf_op jit(solution)/shard_map/ppermute | solution.py:125
  280.8 5.5 %collective-permute-start.20 = (f32[2,32,32]{2,1,0:T(8,128)S(1)}, f32[2,32,32]{2,1,0:T(8,128)S(1)}, u32[]{:S(2)}, u32[]{:S(2)}) collective-permute-start(f32[2,32,32]{2,1,0:T(8,128)S(1)} %add.171), channel_id=1, source_target_pairs={{0,2},{1,3},{2,0},{3,1},{4,6},{5,7},{6,4},{7,5},{8,10},{9,11},{10,... | collective-permute-start | bytes 24584 | tf_op jit(solution)/shard_map/ppermute | solution.py:46
  289.7 3.8 %collective-permute-start.23 = (f32[32,32]{0,1:T(8,128)S(1)}, f32[32,32]{0,1:T(8,128)S(1)}, u32[]{:S(2)}, u32[]{:S(2)}) collective-permute-start(f32[32,32]{0,1:T(8,128)S(1)} %fusion.71), channel_id=1, source_target_pairs={{0,1},{1,0},{2,3},{3,2},{4,5},{5,4},{6,7},{7,6},{8,9},{9,8},{10,11... | collective-permute-start | bytes 12296 | tf_op jit(solution)/shard_map/ppermute | solution.py:46
  293.5 4.6 %collective-permute-start.24 = (f32[32,32]{0,1:T(8,128)S(1)}, f32[32,32]{0,1:T(8,128)S(1)}, u32[]{:S(2)}, u32[]{:S(2)}) collective-permute-start(f32[32,32]{0,1:T(8,128)S(1)} %add.174), channel_id=1, source_target_pairs={{0,2},{1,3},{2,0},{3,1},{4,6},{5,7},{6,4},{7,5},{8,10},{9,11},{10,... | collective-permute-start | bytes 12296 | tf_op jit(solution)/shard_map/ppermute | solution.py:46
  (1 other events, 1.1 us)

commit v3 on v2

--- a/solution.py
+++ b/solution.py
@@ -219,11 +219,11 @@
     )(expression, mexp, s3, s2, s1)
 
 
-def backward(expression, mexp, y):
+def backward(expression, mexp, yt):
     rows, width = expression.shape
-    k = y.shape[1]
+    k = yt.shape[0]
     tr, tw = blocks(rows, width)
-    s3, s2, s1 = stacks(split_outside(jnp.transpose(y)), 0)
+    s3, s2, s1 = stacks(split_outside(yt), 0)
     return pl.pallas_call(
         backward_kernel,
         grid=(width // tw, rows // tr),
@@ -265,12 +265,13 @@
 
     y_start, colsum = forward(expression, mexp, start_t, True)
     start_t = lax.optimization_barrier((start_t, y_start))[0]
-    extra = jnp.concatenate([row_gram(start_t, start_t), jnp.sum(y_start, axis=0)[None, :]], axis=0)
+    y_start = jnp.transpose(y_start)
+    extra = jnp.concatenate([row_gram(start_t, start_t), jnp.sum(y_start, axis=1)[None, :]], axis=0)
     y_start, extra = gene_sum_with(y_start, extra)
     gram0 = extra[:-1]
     lower0 = jnp.linalg.cholesky(gram0)
     current = left_solve(lower0, start_t)
-    y = right_solve(lower0, y_start)
+    y = left_solve(lower0, y_start)
     totals = butterfly_sum(jnp.concatenate([colsum[0], extra[-1]]), "cell")
     means = totals[:width] / cells
     mean_side = right_solve(lower0, (totals[width:] / cells)[None, :])[0]
@@ -281,7 +282,7 @@
     beta_list = []
     for step in range(STEPS):
         if step > 0:
-            y, mean_side = gene_sum_with(forward(expression, mexp, current, False)[0],
+            y, mean_side = gene_sum_with(jnp.transpose(forward(expression, mexp, current, False)[0]),
                                          jnp.dot(current, means, precision=HI))
         part = backward(expression, mexp, y)
         basis = [current] if older is None else [current, older]

time: 308 us -> 311 us (level)
  waiting for transfers between devices: 99.6 us -> 103 us
    ppermute x15, waiting for transfers between devices: 59.1 us -> 62.4 us  [butterfly_sum(): x = x + lax.ppermute(x, axis, [(i, i ^ s) for i in range(n)])]
where the time goes in v3:
time: 311 us; the launch traced here: 310 us
  Pallas kernels  115 us (37%)
  waiting for transfers between devices  103 us (33%)
  other arithmetic  37.8 us (12%)
  starting transfers between devices  27.2 us (9%)
  matrix products  17.9 us (6%)
  local copies, waits for them, and re-layouts  7.63 us (2%)
    pallas_call x2, Pallas kernels, forward(): pl.pallas_call(forward_kernel, grid=(rows // tr, width // tw), in_specs=i...  63.1 us
    ppermute x15, waiting for transfers between devices, butterfly_sum(): x = x + lax.ppermute(x, axis, [(i, i ^ s) for i in range(n)])  62.4 us
    pallas_call x2, Pallas kernels, backward(): pl.pallas_call(backward_kernel, grid=(width // tw, rows // tr), in_specs=...  52.1 us
    ppermute x4, waiting for transfers between devices, cell_image_sum(): lax.ppermute(pack_rows(send, extra), axis, [(i, i ^ s) for i in range(n)])  21.2 us
    ppermute x15, starting transfers between devices, butterfly_sum(): x = x + lax.ppermute(x, axis, [(i, i ^ s) for i in range(n)])  18.1 us
    ppermute x2, waiting for transfers between devices, cell_image_sum(): lax.ppermute(pack_rows(x, extra), axis, [(i, i ^ s) for i in range(n)])  14.7 us
    another operation x5, other arithmetic, left_solve(): return lax.linalg.triangular_solve(lower, x, left_side=True, lower=True)  8.61 us
    dot_general x6, matrix products, row_gram(): lax.dot_general(a, b, (((1,), (1,)), ((), ())), precision=HI, preferred_e...  8.3 us
  transfers between devices with their start and end apart: 25, of which 20 were waited for; matrix products, arithmetic and copies ran while one was open for 1% of the time, Pallas kernels for 0%

profile of v3, /device:TPU:0, one launch (start us, length us, event | category | flops | bytes accessed | tf_op | source)
XLA Modules:
  0.0 310.1 jit_solution(7796055028505854465)
XLA Ops:
  6.2 32.4 %shard_map.58 = (f32[1536,32]{1,0:T(8,128)}, f32[1,8192]{1,0:T(1,128)}) custom-call(f32[1536,8192]{1,0:T(8,128)} %x_ref.7, f32[6,1,8192]{2,1,0:T(1,128)} %broadcast_in_dim_reshape.3.m_ref, bf16[96,8192]{1,0:T(8,128)(2,1)} %pad_maximum_fusion.s3_ref, bf16[64,8192]{1,0:T(8,128)(2,1)} %pad_maximum_fusion.2.s2_ref, bf16[32,8192]{1,0:T(8,128)(2,1)} %copy-done.3), custom_call_target="tpu_custom_call" | custom-call | tf_op jit(solution)/shard_map/pallas_call | solution.py:212
  41.7 3.1 collective-permute-start
  44.8 6.0 %collective-permute-done = f32[33,1536]{1,0:T(8,128)S(1)} collective-permute-done((f32[33,1536]{1,0:T(8,128)S(1)}, f32[33,1536]{1,0:T(8,128)S(1)}, u32[]{:S(2)}, u32[]{:S(2)}) %collective-permute-start) | collective-permute-done | bytes 202784 | tf_op jit(solution)/shard_map/ppermute | solution.py:46
  50.8 2.8 collective-permute-start.1
  53.6 10.6 %collective-permute-done.1 = f32[33,1536]{1,0:T(8,128)S(1)} collective-permute-done((f32[33,1536]{1,0:T(8,128)S(1)}, f32[33,1536]{1,0:T(8,128)S(1)}, u32[]{:S(2)}, u32[]{:S(2)}) %collective-permute-start.1) | collective-permute-done | bytes 202784 | tf_op jit(solution)/shard_map/ppermute | solution.py:46
  64.3 2.9 cholesky.59
  68.6 2.4 custom-call.13
  73.9 26.0 %shard_map.59 = f32[32,8192]{1,0:T(8,128)} custom-call(f32[1536,8192]{1,0:T(8,128)} %x_ref.7, f32[6,1,8192]{2,1,0:T(1,128)} %broadcast_in_dim_reshape.3.m_ref, bf16[96,1536]{1,0:T(8,128)(2,1)} %pad_maximum_fusion.10.s3_ref, bf16[64,1536]{1,0:T(8,128)(2,1)} %pad_maximum_fusion.14.s2_ref, bf16[32,1536]{1,0:T(8,128)(2,1)} %copy-done.6), custom_call_target="tpu_custom_call" | custom-call | tf_op jit(solution)/shard_map/pallas_call | solution.py:227
  109.3 8.4 %collective-permute-done.3 = f32[33,2048]{1,0:T(8,128)S(1)} collective-permute-done((f32[33,2048]{1,0:T(8,128)S(1)}, f32[33,2048]{1,0:T(8,128)S(1)}, u32[]{:S(2)}, u32[]{:S(2)}) %collective-permute-start.3) | collective-permute-done | bytes 270368 | tf_op jit(solution)/shard_map/ppermute | solution.py:112
  119.5 7.5 %collective-permute-done.4 = f32[33,2048]{1,0:T(8,128)S(1)} collective-permute-done((f32[33,2048]{1,0:T(8,128)S(1)}, f32[33,2048]{1,0:T(8,128)S(1)}, u32[]{:S(2)}, u32[]{:S(2)}) %collective-permute-start.4) | collective-permute-done | bytes 270368 | tf_op jit(solution)/shard_map/ppermute | solution.py:119
  129.2 5.3 %collective-permute-done.8 = f32[8224]{0:T(1024)S(1)} collective-permute-done((f32[8224]{0:T(1024)S(1)}, f32[8224]{0:T(1024)S(1)}, u32[]{:S(2)}, u32[]{:S(2)}) %collective-permute-start.8) | collective-permute-done | bytes 32928 | tf_op jit(solution)/shard_map/ppermute | solution.py:46
  135.8 2.6 collective-permute-done.9
  139.2 3.2 %collective-permute-done.5 = f32[1,32,32]{2,1,0:T(8,128)S(1)} collective-permute-done((f32[1,32,32]{2,1,0:T(8,128)S(1)}, f32[1,32,32]{2,1,0:T(8,128)S(1)}, u32[]{:S(2)}, u32[]{:S(2)}) %collective-permute-start.5) | collective-permute-done | bytes 4128 | tf_op jit(solution)/shard_map/ppermute | solution.py:46
  144.5 2.6 collective-permute-done.6
  150.4 2.8 collective-permute-done.12
  155.2 2.6 collective-permute-done.13
  157.9 2.9 cholesky.70
  162.1 2.4 custom-call.14
  169.2 30.7 %shard_map.60 = f32[1536,32]{1,0:T(8,128)} custom-call(f32[1536,8192]{1,0:T(8,128)} %x_ref.7, f32[6,1,8192]{2,1,0:T(1,128)} %broadcast_in_dim_reshape.3.m_ref, bf16[96,8192]{1,0:T(8,128)(2,1)} %pad_maximum_fusion.1.s3_ref, bf16[64,8192]{1,0:T(8,128)(2,1)} %pad_maximum_fusion.3.s2_ref, bf16[32,8192]{1,0:T(8,128)(2,1)} %copy-done.4), custom_call_target="tpu_custom_call" | custom-call | tf_op jit(solution)/shard_map/pallas_call | solution.py:212
  202.3 7.8 %collective-permute-done.14 = f32[33,1536]{1,0:T(8,128)S(1)} collective-permute-done((f32[33,1536]{1,0:T(8,128)S(1)}, f32[33,1536]{1,0:T(8,128)S(1)}, u32[]{:S(2)}, u32[]{:S(2)}) %collective-permute-start.14) | collective-permute-done | bytes 202784 | tf_op jit(solution)/shard_map/ppermute | solution.py:46
  212.0 7.2 %collective-permute-done.15 = f32[33,1536]{1,0:T(8,128)S(1)} collective-permute-done((f32[33,1536]{1,0:T(8,128)S(1)}, f32[33,1536]{1,0:T(8,128)S(1)}, u32[]{:S(2)}, u32[]{:S(2)}) %collective-permute-start.15) | collective-permute-done | bytes 202784 | tf_op jit(solution)/shard_map/ppermute | solution.py:46
  220.7 26.0 %shard_map.61 = f32[32,8192]{1,0:T(8,128)} custom-call(f32[1536,8192]{1,0:T(8,128)} %x_ref.7, f32[6,1,8192]{2,1,0:T(1,128)} %broadcast_in_dim_reshape.3.m_ref, bf16[96,1536]{1,0:T(8,128)(2,1)} %pad_maximum_fusion.11.s3_ref, bf16[64,1536]{1,0:T(8,128)(2,1)} %pad_maximum_fusion.15.s2_ref, bf16[32,1536]{1,0:T(8,128)(2,1)} %copy-done.7), custom_call_target="tpu_custom_call" | custom-call | tf_op jit(solution)/shard_map/pallas_call | solution.py:227
  246.8 2.3 convolution_bitcast_fusion
  253.0 2.4 collective-permute-done.16
  258.9 8.2 %collective-permute-done.17 = f32[33,2048]{1,0:T(8,128)S(1)} collective-permute-done((f32[33,2048]{1,0:T(8,128)S(1)}, f32[33,2048]{1,0:T(8,128)S(1)}, u32[]{:S(2)}, u32[]{:S(2)}) %collective-permute-start.17) | collective-permute-done | bytes 270368 | tf_op jit(solution)/shard_map/ppermute | solution.py:112
  269.0 7.3 %collective-permute-done.18 = f32[33,2048]{1,0:T(8,128)S(1)} collective-permute-done((f32[33,2048]{1,0:T(8,128)S(1)}, f32[33,2048]{1,0:T(8,128)S(1)}, u32[]{:S(2)}, u32[]{:S(2)}) %collective-permute-start.18) | collective-permute-done | bytes 270368 | tf_op jit(solution)/shard_map/ppermute | solution.py:119
  278.2 4.8 %collective-permute-done.21 = f32[32,2048]{1,0:T(8,128)S(1)} collective-permute-done((f32[32,2048]{1,0:T(8,128)S(1)}, f32[32,2048]{1,0:T(8,128)S(1)}, u32[]{:S(2)}, u32[]{:S(2)}) %collective-permute-start.21) | collective-permute-done | bytes 262176 | tf_op jit(solution)/shard_map/ppermute | solution.py:125
  283.4 5.2 %collective-permute-done.20 = f32[2,32,32]{2,1,0:T(8,128)S(1)} collective-permute-done((f32[2,32,32]{2,1,0:T(8,128)S(1)}, f32[2,32,32]{2,1,0:T(8,128)S(1)}, u32[]{:S(2)}, u32[]{:S(2)}) %collective-permute-start.20) | collective-permute-done | bytes 8224 | tf_op jit(solution)/shard_map/ppermute | solution.py:46
  292.5 3.4 %collective-permute-done.23 = f32[32,32]{0,1:T(8,128)S(1)} collective-permute-done((f32[32,32]{0,1:T(8,128)S(1)}, f32[32,32]{0,1:T(8,128)S(1)}, u32[]{:S(2)}, u32[]{:S(2)}) %collective-permute-start.23) | collective-permute-done | bytes 4128 | tf_op jit(solution)/shard_map/ppermute | solution.py:46
  297.4 3.1 %collective-permute-done.24 = f32[32,32]{0,1:T(8,128)S(1)} collective-permute-done((f32[32,32]{0,1:T(8,128)S(1)}, f32[32,32]{0,1:T(8,128)S(1)}, u32[]{:S(2)}, u32[]{:S(2)}) %collective-permute-start.24) | collective-permute-done | bytes 4128 | tf_op jit(solution)/shard_map/ppermute | solution.py:46
  300.6 2.9 cholesky.81
  304.9 2.4 custom-call.15
  (175 shorter events, 68.5 us)
Async XLA Ops:
  6.2 33.9 %copy-start = (f32[8192,32]{0,1:T(8,128)S(1)}, f32[8192,32]{0,1:T(8,128)}, u32[]{:S(2)}) copy-start(f32[8192,32]{0,1:T(8,128)} %param.8) | copy-start | bytes 3145732
  38.6 2.8 copy-start.5
  41.7 9.0 %collective-permute-start = (f32[33,1536]{1,0:T(8,128)S(1)}, f32[33,1536]{1,0:T(8,128)S(1)}, u32[]{:S(2)}, u32[]{:S(2)}) collective-permute-start(f32[33,1536]{1,0:T(8,128)S(1)} %pad_maximum_fusion.12), channel_id=1, source_target_pairs={{0,1},{1,0},{2,3},{3,2},{4,5},{5,4},{6,7},{7,6},{8,9},{9,8},{10,11... | collective-permute-start | bytes 608264 | tf_op jit(solution)/shard_map/ppermute | solution.py:46
  50.8 13.4 %collective-permute-start.1 = (f32[33,1536]{1,0:T(8,128)S(1)}, f32[33,1536]{1,0:T(8,128)S(1)}, u32[]{:S(2)}, u32[]{:S(2)}) collective-permute-start(f32[33,1536]{1,0:T(8,128)S(1)} %fusion.67), channel_id=1, source_target_pairs={{0,2},{1,3},{2,0},{3,1},{4,6},{5,7},{6,4},{7,5},{8,10},{9,11},{10,... | collective-permute-start | bytes 608264 | tf_op jit(solution)/shard_map/ppermute | solution.py:46
  71.5 2.5 copy-start.6
  100.0 6.8 %copy-start.2 = (f32[32,8192]{1,0:T(8,128)S(1)}, f32[32,8192]{1,0:T(8,128)}, u32[]{:S(2)}) copy-start(f32[32,8192]{1,0:T(8,128)} %shard_map.59) | copy-start | bytes 3145732
  103.5 2.3 collective-permute-start.2
  106.7 12.7 %copy-start.8 = (f32[1,8192]{1,0:T(1,128)S(1)}, f32[1,8192]{1,0:T(1,128)}, u32[]{:S(2)}) copy-start(f32[1,8192]{1,0:T(1,128)} %get-tuple-element.10) | copy-start | bytes 98308
  107.9 9.8 %collective-permute-start.3 = (f32[33,2048]{1,0:T(8,128)S(1)}, f32[33,2048]{1,0:T(8,128)S(1)}, u32[]{:S(2)}, u32[]{:S(2)}) collective-permute-start(f32[33,2048]{1,0:T(8,128)S(1)} %pad_maximum_fusion.6), channel_id=1, source_target_pairs={{0,8},{4,12},{8,0},{12,4},{16,24},{20,28},{24,16},{28,20},{1,9},{5... | collective-permute-start | bytes 811016 | tf_op jit(solution)/shard_map/ppermute | solution.py:112
  118.0 9.0 %collective-permute-start.4 = (f32[33,2048]{1,0:T(8,128)S(1)}, f32[33,2048]{1,0:T(8,128)S(1)}, u32[]{:S(2)}, u32[]{:S(2)}) collective-permute-start(f32[33,2048]{1,0:T(8,128)S(1)} %pad_maximum_fusion.7), channel_id=1, source_target_pairs={{0,16},{4,20},{8,24},{12,28},{16,0},{20,4},{24,8},{28,12},{1,17},{... | collective-permute-start | bytes 811016 | tf_op jit(solution)/shard_map/ppermute | solution.py:119
  119.4 9.0 %collective-permute-start.7 = (f32[8224]{0:T(1024)S(1)}, f32[8224]{0:T(1024)S(1)}, u32[]{:S(2)}, u32[]{:S(2)}) collective-permute-start(f32[8224]{0:T(1024)S(1)} %pad_maximum_fusion.16), channel_id=1, source_target_pairs={{0,4},{4,0},{8,12},{12,8},{16,20},{20,16},{24,28},{28,24},{1,5},{5... | collective-permute-start | bytes 98696 | tf_op jit(solution)/shard_map/ppermute | solution.py:46
  127.0 11.5 %collective-permute-start.10 = (f32[32,2048]{1,0:T(8,128)S(1)}, f32[32,2048]{1,0:T(8,128)S(1)}, u32[]{:S(2)}, u32[]{:S(2)}) collective-permute-start(f32[32,2048]{1,0:T(8,128)S(1)} %slice_add_fusion.4), channel_id=1, source_target_pairs={{0,8},{4,12},{8,0},{12,4},{16,24},{20,28},{24,16},{28,20},{1,9},{5... | collective-permute-start | bytes 786440 | tf_op jit(solution)/shard_map/ppermute | solution.py:125
  128.4 6.0 %collective-permute-start.8 = (f32[8224]{0:T(1024)S(1)}, f32[8224]{0:T(1024)S(1)}, u32[]{:S(2)}, u32[]{:S(2)}) collective-permute-start(f32[8224]{0:T(1024)S(1)} %fusion.65), channel_id=1, source_target_pairs={{0,8},{4,12},{8,0},{12,4},{16,24},{20,28},{24,16},{28,20},{1,9},{5... | collective-permute-start | bytes 98696 | tf_op jit(solution)/shard_map/ppermute | solution.py:46
  134.5 4.0 %collective-permute-start.9 = (f32[8224]{0:T(1024)S(1)}, f32[8224]{0:T(1024)S(1)}, u32[]{:S(2)}, u32[]{:S(2)}) collective-permute-start(f32[8224]{0:T(1024)S(1)} %add.161), channel_id=1, source_target_pairs={{0,16},{4,20},{8,24},{12,28},{16,0},{20,4},{24,8},{28,12},{1,17},{... | collective-permute-start | bytes 98696 | tf_op jit(solution)/shard_map/ppermute | solution.py:46
  138.6 8.5 %collective-permute-start.11 = (f32[32,4096]{1,0:T(8,128)S(1)}, f32[32,4096]{1,0:T(8,128)S(1)}, u32[]{:S(2)}, u32[]{:S(2)}) collective-permute-start(f32[32,4096]{1,0:T(8,128)S(1)} %maximum_select_fusion.2), channel_id=1, source_target_pairs={{0,4},{4,0},{8,12},{12,8},{16,20},{20,16},{24,28},{28,24},{1,5},{5... | collective-permute-start | bytes 1572872 | tf_op jit(solution)/shard_map/ppermute | solution.py:125
  138.7 3.8 %collective-permute-start.5 = (f32[1,32,32]{2,1,0:T(8,128)S(1)}, f32[1,32,32]{2,1,0:T(8,128)S(1)}, u32[]{:S(2)}, u32[]{:S(2)}) collective-permute-start(f32[1,32,32]{2,1,0:T(8,128)S(1)} %add_bitcast_fusion), channel_id=1, source_target_pairs={{0,1},{1,0},{2,3},{3,2},{4,5},{5,4},{6,7},{7,6},{8,9},{9,8},{10,11... | collective-permute-start | bytes 12296 | tf_op jit(solution)/shard_map/ppermute | solution.py:46
  142.5 4.6 %collective-permute-start.6 = (f32[1,32,32]{2,1,0:T(8,128)S(1)}, f32[1,32,32]{2,1,0:T(8,128)S(1)}, u32[]{:S(2)}, u32[]{:S(2)}) collective-permute-start(f32[1,32,32]{2,1,0:T(8,128)S(1)} %add.158), channel_id=1, source_target_pairs={{0,2},{1,3},{2,0},{3,1},{4,6},{5,7},{6,4},{7,5},{8,10},{9,11},{10,... | collective-permute-start | bytes 12296 | tf_op jit(solution)/shard_map/ppermute | solution.py:46
  144.5 4.9 %copy-start.9 = (f32[32]{0:T(128)}, f32[32]{0:T(128)S(1)}, u32[]{:S(2)}) copy-start(f32[32]{0:T(128)S(1)} %convolution_bitcast_fusion.3) | copy-start | bytes 388
  149.3 3.8 %collective-permute-start.12 = (f32[32,32]{0,1:T(8,128)S(1)}, f32[32,32]{0,1:T(8,128)S(1)}, u32[]{:S(2)}, u32[]{:S(2)}) collective-permute-start(f32[32,32]{0,1:T(8,128)S(1)} %fusion.70), channel_id=1, source_target_pairs={{0,1},{1,0},{2,3},{3,2},{4,5},{5,4},{6,7},{7,6},{8,9},{9,8},{10,11... | collective-permute-start | bytes 12296 | tf_op jit(solution)/shard_map/ppermute | solution.py:46
  153.1 4.6 %collective-permute-start.13 = (f32[32,32]{0,1:T(8,128)S(1)}, f32[32,32]{0,1:T(8,128)S(1)}, u32[]{:S(2)}, u32[]{:S(2)}) collective-permute-start(f32[32,32]{0,1:T(8,128)S(1)} %add.164), channel_id=1, source_target_pairs={{0,2},{1,3},{2,0},{3,1},{4,6},{5,7},{6,4},{7,5},{8,10},{9,11},{10,... | collective-permute-start | bytes 12296 | tf_op jit(solution)/shard_map/ppermute | solution.py:46
  201.3 8.8 %collective-permute-start.14 = (f32[33,1536]{1,0:T(8,128)S(1)}, f32[33,1536]{1,0:T(8,128)S(1)}, u32[]{:S(2)}, u32[]{:S(2)}) collective-permute-start(f32[33,1536]{1,0:T(8,128)S(1)} %pad_maximum_fusion.13), channel_id=1, source_target_pairs={{0,1},{1,0},{2,3},{3,2},{4,5},{5,4},{6,7},{7,6},{8,9},{9,8},{10,11... | collective-permute-start | bytes 608264 | tf_op jit(solution)/shard_map/ppermute | solution.py:46
  210.1 9.1 %collective-permute-start.15 = (f32[33,1536]{1,0:T(8,128)S(1)}, f32[33,1536]{1,0:T(8,128)S(1)}, u32[]{:S(2)}, u32[]{:S(2)}) collective-permute-start(f32[33,1536]{1,0:T(8,128)S(1)} %fusion.66), channel_id=1, source_target_pairs={{0,2},{1,3},{2,0},{3,1},{4,6},{5,7},{6,4},{7,5},{8,10},{9,11},{10,... | collective-permute-start | bytes 608264 | tf_op jit(solution)/shard_map/ppermute | solution.py:46
  252.9 2.4 collective-permute-start.16
  256.5 26.7 %copy-start.10 = (f32[32]{0:T(128)S(1)}, f32[32]{0:T(128)}, u32[]{:S(2)}) copy-start(f32[32]{0:T(128)} %copy-done.9) | copy-start | bytes 388
  257.4 9.8 %collective-permute-start.17 = (f32[33,2048]{1,0:T(8,128)S(1)}, f32[33,2048]{1,0:T(8,128)S(1)}, u32[]{:S(2)}, u32[]{:S(2)}) collective-permute-start(f32[33,2048]{1,0:T(8,128)S(1)} %pad_maximum_fusion.8), channel_id=1, source_target_pairs={{0,8},{4,12},{8,0},{12,4},{16,24},{20,28},{24,16},{28,20},{1,9},{5... | collective-permute-start | bytes 811016 | tf_op jit(solution)/shard_map/ppermute | solution.py:112
  267.3 9.0 %collective-permute-start.18 = (f32[33,2048]{1,0:T(8,128)S(1)}, f32[33,2048]{1,0:T(8,128)S(1)}, u32[]{:S(2)}, u32[]{:S(2)}) collective-permute-start(f32[33,2048]{1,0:T(8,128)S(1)} %pad_maximum_fusion.9), channel_id=1, source_target_pairs={{0,16},{4,20},{8,24},{12,28},{16,0},{20,4},{24,8},{28,12},{1,17},{... | collective-permute-start | bytes 811016 | tf_op jit(solution)/shard_map/ppermute | solution.py:119
  276.3 6.7 %collective-permute-start.21 = (f32[32,2048]{1,0:T(8,128)S(1)}, f32[32,2048]{1,0:T(8,128)S(1)}, u32[]{:S(2)}, u32[]{:S(2)}) collective-permute-start(f32[32,2048]{1,0:T(8,128)S(1)} %slice_add_fusion.2), channel_id=1, source_target_pairs={{0,8},{4,12},{8,0},{12,4},{16,24},{20,28},{24,16},{28,20},{1,9},{5... | collective-permute-start | bytes 786440 | tf_op jit(solution)/shard_map/ppermute | solution.py:125
  278.0 5.2 %collective-permute-start.19 = (f32[2,32,32]{2,1,0:T(8,128)S(1)}, f32[2,32,32]{2,1,0:T(8,128)S(1)}, u32[]{:S(2)}, u32[]{:S(2)}) collective-permute-start(f32[2,32,32]{2,1,0:T(8,128)S(1)} %add_add_fusion), channel_id=1, source_target_pairs={{0,1},{1,0},{2,3},{3,2},{4,5},{5,4},{6,7},{7,6},{8,9},{9,8},{10,11... | collective-permute-start | bytes 24584 | tf_op jit(solution)/shard_map/ppermute | solution.py:46
  283.0 6.8 %collective-permute-start.22 = (f32[32,4096]{1,0:T(8,128)S(1)}, f32[32,4096]{1,0:T(8,128)S(1)}, u32[]{:S(2)}, u32[]{:S(2)}) collective-permute-start(f32[32,4096]{1,0:T(8,128)S(1)} %maximum_select_fusion.3), channel_id=1, source_target_pairs={{0,4},{4,0},{8,12},{12,8},{16,20},{20,16},{24,28},{28,24},{1,5},{5... | collective-permute-start | bytes 1572872 | tf_op jit(solution)/shard_map/ppermute | solution.py:125
  283.2 5.5 %collective-permute-start.20 = (f32[2,32,32]{2,1,0:T(8,128)S(1)}, f32[2,32,32]{2,1,0:T(8,128)S(1)}, u32[]{:S(2)}, u32[]{:S(2)}) collective-permute-start(f32[2,32,32]{2,1,0:T(8,128)S(1)} %add.175), channel_id=1, source_target_pairs={{0,2},{1,3},{2,0},{3,1},{4,6},{5,7},{6,4},{7,5},{8,10},{9,11},{10,... | collective-permute-start | bytes 24584 | tf_op jit(solution)/shard_map/ppermute | solution.py:46
  292.1 3.8 %collective-permute-start.23 = (f32[32,32]{0,1:T(8,128)S(1)}, f32[32,32]{0,1:T(8,128)S(1)}, u32[]{:S(2)}, u32[]{:S(2)}) collective-permute-start(f32[32,32]{0,1:T(8,128)S(1)} %fusion.71), channel_id=1, source_target_pairs={{0,1},{1,0},{2,3},{3,2},{4,5},{5,4},{6,7},{7,6},{8,9},{9,8},{10,11... | collective-permute-start | bytes 12296 | tf_op jit(solution)/shard_map/ppermute | solution.py:46
  295.9 4.6 %collective-permute-start.24 = (f32[32,32]{0,1:T(8,128)S(1)}, f32[32,32]{0,1:T(8,128)S(1)}, u32[]{:S(2)}, u32[]{:S(2)}) collective-permute-start(f32[32,32]{0,1:T(8,128)S(1)} %add.178), channel_id=1, source_target_pairs={{0,2},{1,3},{2,0},{3,1},{4,6},{5,7},{6,4},{7,5},{8,10},{9,11},{10,... | collective-permute-start | bytes 12296 | tf_op jit(solution)/shard_map/ppermute | solution.py:46
  (4 other events, 8.1 us)

commit v4 on v3

--- a/solution.py
+++ b/solution.py
@@ -167,7 +167,7 @@
             c_ref[:, sl] += s
 
 
-def backward_kernel(x_ref, m_ref, s3_ref, s2_ref, s1_ref, o_ref):
+def backward_kernel(x_ref, m_ref, s3_ref, s2_ref, s1_ref, *refs):
     i = pl.program_id(1)
     k = s1_ref.shape[0]
     x = x_ref[...] * m_ref[0]
@@ -176,10 +176,14 @@
     c = jnp.dot(s2_ref[...], x2, preferred_element_type=F32)
     d = jnp.dot(s1_ref[...], x3, preferred_element_type=F32)
     part = ((a[2 * k:] + c[k:] + d) + (a[k:2 * k] + c[:k])) + a[:k]
+    o_ref = refs[-1]
 
     @pl.when(i == 0)
     def _():
-        o_ref[...] = part
+        if len(refs) == 2:
+            o_ref[...] = refs[0][...] + part
+        else:
+            o_ref[...] = part
 
     @pl.when(i > 0)
     def _():
@@ -192,26 +196,27 @@
     return tr, tw
 
 
-def forward(expression, mexp, bt, with_colsum):
+def forward(expression, mexp, bt, with_colsum, lo, count):
     rows, width = expression.shape
     k = bt.shape[0]
     tr, tw = blocks(rows, width)
+    off = lo // tr
     s3, s2, s1 = stacks(split_outside(bt), 0)
     in_specs = [
-        pl.BlockSpec((tr, tw), lambda i, j: (i, j)),
-        pl.BlockSpec((1, 1, tw), lambda i, j: (i, 0, j)),
+        pl.BlockSpec((tr, tw), lambda i, j: (i + off, j)),
+        pl.BlockSpec((1, 1, tw), lambda i, j: (i + off, 0, j)),
         pl.BlockSpec((3 * k, tw), lambda i, j: (0, j)),
         pl.BlockSpec((2 * k, tw), lambda i, j: (0, j)),
         pl.BlockSpec((k, tw), lambda i, j: (0, j)),
     ]
     out_specs = [pl.BlockSpec((tr, k), lambda i, j: (i, 0))]
-    out_shape = [jax.ShapeDtypeStruct((rows, k), F32)]
+    out_shape = [jax.ShapeDtypeStruct((count, k), F32)]
     if with_colsum:
         out_specs.append(pl.BlockSpec((1, width), lambda i, j: (0, 0)))
         out_shape.append(jax.ShapeDtypeStruct((1, width), F32))
     return pl.pallas_call(
         forward_kernel,
-        grid=(rows // tr, width // tw),
+        grid=(count // tr, width // tw),
         in_specs=in_specs,
         out_specs=out_specs,
         out_shape=out_shape,
@@ -219,25 +224,31 @@
     )(expression, mexp, s3, s2, s1)
 
 
-def backward(expression, mexp, yt):
+def backward(expression, mexp, yt, lo, init=None):
     rows, width = expression.shape
-    k = yt.shape[0]
+    k, count = yt.shape
     tr, tw = blocks(rows, width)
+    off = lo // tr
     s3, s2, s1 = stacks(split_outside(yt), 0)
+    in_specs = [
+        pl.BlockSpec((tr, tw), lambda j, i: (i + off, j)),
+        pl.BlockSpec((1, 1, tw), lambda j, i: (i + off, 0, j)),
+        pl.BlockSpec((3 * k, tr), lambda j, i: (0, i)),
+        pl.BlockSpec((2 * k, tr), lambda j, i: (0, i)),
+        pl.BlockSpec((k, tr), lambda j, i: (0, i)),
+    ]
+    args = [expression, mexp, s3, s2, s1]
+    if init is not None:
+        in_specs.append(pl.BlockSpec((k, tw), lambda j, i: (0, j)))
+        args.append(init)
     return pl.pallas_call(
         backward_kernel,
-        grid=(width // tw, rows // tr),
-        in_specs=[
-            pl.BlockSpec((tr, tw), lambda j, i: (i, j)),
-            pl.BlockSpec((1, 1, tw), lambda j, i: (i, 0, j)),
-            pl.BlockSpec((3 * k, tr), lambda j, i: (0, i)),
-            pl.BlockSpec((2 * k, tr), lambda j, i: (0, i)),
-            pl.BlockSpec((k, tr), lambda j, i: (0, i)),
-        ],
+        grid=(width // tw, count // tr),
+        in_specs=in_specs,
         out_specs=pl.BlockSpec((k, tw), lambda j, i: (0, j)),
         out_shape=jax.ShapeDtypeStruct((k, width), F32),
         compiler_params=pltpu.CompilerParams(dimension_semantics=("arbitrary", "arbitrary")),
-    )(expression, mexp, s3, s2, s1)
+    )(*args)
 
 
 HI = lax.Precision.HIGHEST
@@ -253,6 +264,12 @@
 
 def right_solve(lower, x):
     return lax.linalg.triangular_solve(lower, x, left_side=False, lower=True, transpose_a=True)
+
+
+def row_halves(rows):
+    tiles = rows // TILE
+    first = (tiles + 1) // 2 * TILE
+    return [(0, first), (first, rows - first)] if first < rows else [(0, rows)]
 
 
 def per_device(expression, tile_mask, start):
@@ -262,17 +279,29 @@
     cells = rows * cell_count
     mexp = jnp.repeat(tile_mask.astype(F32), TILE, axis=1)[:, None, :]
     start_t = jnp.transpose(start)
-
-    y_start, colsum = forward(expression, mexp, start_t, True)
-    start_t = lax.optimization_barrier((start_t, y_start))[0]
-    y_start = jnp.transpose(y_start)
-    extra = jnp.concatenate([row_gram(start_t, start_t), jnp.sum(y_start, axis=1)[None, :]], axis=0)
-    y_start, extra = gene_sum_with(y_start, extra)
-    gram0 = extra[:-1]
+    halves = row_halves(rows)
+
+    ys = []
+    colsum = 0.0
+    row_total = 0.0
+    for h, (lo, count) in enumerate(halves):
+        y_h, c_h = forward(expression, mexp, start_t, True, lo, count)
+        colsum = colsum + c_h[0]
+        y_h = jnp.transpose(y_h)
+        if h == 0:
+            start_t = lax.optimization_barrier((start_t, y_h))[0]
+            extra = jnp.concatenate([row_gram(start_t, start_t), jnp.sum(y_h, axis=1)[None, :]], axis=0)
+            y_h, extra = gene_sum_with(y_h, extra)
+            gram0 = extra[:-1]
+            row_total = row_total + extra[-1]
+        else:
+            y_h, extra = gene_sum_with(y_h, jnp.sum(y_h, axis=1))
+            row_total = row_total + extra
+        ys.append(y_h)
     lower0 = jnp.linalg.cholesky(gram0)
     current = left_solve(lower0, start_t)
-    y = left_solve(lower0, y_start)
-    totals = butterfly_sum(jnp.concatenate([colsum[0], extra[-1]]), "cell")
+    ys = [left_solve(lower0, y_h) for y_h in ys]
+    totals = butterfly_sum(jnp.concatenate([colsum, row_total]), "cell")
     means = totals[:width] / cells
     mean_side = right_solve(lower0, (totals[width:] / cells)[None, :])[0]
 
@@ -282,9 +311,17 @@
     beta_list = []
     for step in range(STEPS):
         if step > 0:
-            y, mean_side = gene_sum_with(jnp.transpose(forward(expression, mexp, current, False)[0]),
-                                         jnp.dot(current, means, precision=HI))
-        part = backward(expression, mexp, y)
+            ys = []
+            for h, (lo, count) in enumerate(halves):
+                y_h = jnp.transpose(forward(expression, mexp, current, False, lo, count)[0])
+                if h == 0:
+                    y_h, mean_side = gene_sum_with(y_h, jnp.dot(current, means, precision=HI))
+                else:
+                    y_h = butterfly_sum(y_h, "gene")
+                ys.append(y_h)
+        part = None
+        for (lo, count), y_h in zip(halves, ys):
+            part = backward(expression, mexp, y_h, lo, part)
         basis = [current] if older is None else [current, older]
         sides = [mean_side] if older is None else [mean_side, older_side]
         proj_part = jnp.stack([row_gram(v, part) for v in basis])

time: 311 us -> 317 us (1.019)
  waiting for transfers between devices: 103 us -> 80.7 us
  Pallas kernels: 115 us -> 126 us
  starting transfers between devices: 27.2 us -> 36.5 us
  other arithmetic: 37.8 us -> 45 us
    ppermute x15 -> x19, waiting for transfers between devices: 62.4 us -> 42.7 us  [butterfly_sum(): x = x + lax.ppermute(x, axis, [(i, i ^ s) for i in range(n)])]
    pallas_call x4 -> x8, Pallas kernels: 115 us -> 126 us  [the longest x4 68.7 us: forward(): pl.pallas_call(forward_kernel, grid=(count // tr, width // tw), in_specs=...]
    ppermute x15 -> x19, starting transfers between devices: 18.1 us -> 27.1 us  [butterfly_sum(): x = x + lax.ppermute(x, axis, [(i, i ^ s) for i in range(n)])]
    concatenate x4 -> x7, other arithmetic: 4.01 us -> 6.5 us  [stacks(): jnp.concatenate(p, axis=axis)]
  transfers between devices with their start and end apart: 25 -> 29, of which waited for: 20 -> 22; matrix products, arithmetic and copies ran while one was open for 1% -> 4% of each run, Pallas kernels for 0% -> 6%
where the time goes in v4:
time: 317 us; the launch traced here: 316 us
  Pallas kernels  126 us (40%)
  waiting for transfers between devices  80.7 us (25%)
  other arithmetic  45 us (14%)
  starting transfers between devices  36.5 us (12%)
  matrix products  18.2 us (6%)
  local copies, waits for them, and re-layouts  8.72 us (3%)
    pallas_call x4, Pallas kernels, forward(): pl.pallas_call(forward_kernel, grid=(count // tr, width // tw), in_specs=...  68.7 us
    pallas_call x4, Pallas kernels, backward(): pl.pallas_call(backward_kernel, grid=(width // tw, count // tr), in_specs...  57.2 us
    ppermute x19, waiting for transfers between devices, butterfly_sum(): x = x + lax.ppermute(x, axis, [(i, i ^ s) for i in range(n)])  42.7 us
    ppermute x19, starting transfers between devices, butterfly_sum(): x = x + lax.ppermute(x, axis, [(i, i ^ s) for i in range(n)])  27.1 us
    ppermute x4, waiting for transfers between devices, cell_image_sum(): lax.ppermute(pack_rows(send, extra), axis, [(i, i ^ s) for i in range(n)])  20.1 us
    ppermute x2, waiting for transfers between devices, cell_image_sum(): lax.ppermute(pack_rows(x, extra), axis, [(i, i ^ s) for i in range(n)])  14.9 us
    another operation x5, other arithmetic, left_solve(): return lax.linalg.triangular_solve(lower, x, left_side=True, lower=True)  8.61 us
    dot_general x6, matrix products, row_gram(): lax.dot_general(a, b, (((1,), (1,)), ((), ())), precision=HI, preferred_e...  8.39 us
  transfers between devices with their start and end apart: 29, of which 22 were waited for; matrix products, arithmetic and copies ran while one was open for 4% of the time, Pallas kernels for 6%

profile of v4, /device:TPU:0, one launch (start us, length us, event | category | flops | bytes accessed | tf_op | source)
XLA Modules:
  0.0 316.3 jit_solution(8400869111795738377)
XLA Ops:
  6.2 17.7 %shard_map.58 = (f32[768,32]{1,0:T(8,128)}, f32[1,8192]{1,0:T(1,128)}) custom-call(f32[1536,8192]{1,0:T(8,128)} %x_ref.15, f32[6,1,8192]{2,1,0:T(1,128)} %broadcast_in_dim_reshape.3.m_ref, bf16[96,8192]{1,0:T(8,128)(2,1)} %pad_maximum_fusion.s3_ref, bf16[64,8192]{1,0:T(8,128)(2,1)} %pad_maximum_fusion.3.s2_ref, bf16[32,8192]{1,0:T(8,128)(2,1)} %copy-done.4), custom_call_target="tpu_custom_call" | custom-call | tf_op jit(solution)/shard_map/pallas_call | solution.py:217
  27.5 3.1 collective-permute-start
  33.3 17.6 %shard_map.59 = (f32[768,32]{1,0:T(8,128)}, f32[1,8192]{1,0:T(1,128)}) custom-call(f32[1536,8192]{1,0:T(8,128)} %x_ref.15, f32[6,1,8192]{2,1,0:T(1,128)} %broadcast_in_dim_reshape.3.m_ref, bf16[96,8192]{1,0:T(8,128)(2,1)} %pad_maximum_fusion.1.s3_ref, bf16[64,8192]{1,0:T(8,128)(2,1)} %pad_maximum_fusion.4.s2_ref, bf16[32,8192]{1,0:T(8,128)(2,1)} %copy-done.5), custom_call_target="tpu_custom_call" | custom-call | tf_op jit(solution)/shard_map/pallas_call | solution.py:217
  53.3 3.1 collective-permute-start.1
  56.4 4.3 %collective-permute-done.2 = f32[33,768]{1,0:T(8,128)S(1)} collective-permute-done((f32[33,768]{1,0:T(8,128)S(1)}, f32[33,768]{1,0:T(8,128)S(1)}, u32[]{:S(2)}, u32[]{:S(2)}) %collective-permute-start.2) | collective-permute-done | bytes 101408 | tf_op jit(solution)/shard_map/ppermute | solution.py:46
  62.2 5.8 %collective-permute-done.3 = f32[33,768]{1,0:T(8,128)S(1)} collective-permute-done((f32[33,768]{1,0:T(8,128)S(1)}, f32[33,768]{1,0:T(8,128)S(1)}, u32[]{:S(2)}, u32[]{:S(2)}) %collective-permute-start.3) | collective-permute-done | bytes 101408 | tf_op jit(solution)/shard_map/ppermute | solution.py:46
  68.2 2.9 cholesky.59
  72.5 2.4 custom-call.15
  79.3 14.2 %shard_map.60.refs_0_ = f32[32,8192]{1,0:T(8,128)} custom-call(f32[1536,8192]{1,0:T(8,128)} %x_ref.15, f32[6,1,8192]{2,1,0:T(1,128)} %broadcast_in_dim_reshape.3.m_ref, bf16[96,768]{1,0:T(8,128)(2,1)} %pad_maximum_fusion.13.s3_ref, bf16[64,768]{1,0:T(8,128)(2,1)} %pad_maximum_fusion.20.s2_ref, bf16[32,768]{1,0:T(8,128)(2,1)} %copy-done.7), custom_call_target="tpu_custom_call" | custom-call | tf_op jit(solution)/shard_map/pallas_call | solution.py:244
  93.4 14.5 %shard_map.61 = f32[32,8192]{1,0:T(8,128)} custom-call(f32[1536,8192]{1,0:T(8,128)} %x_ref.15, f32[6,1,8192]{2,1,0:T(1,128)} %broadcast_in_dim_reshape.3.m_ref, bf16[96,768]{1,0:T(8,128)(2,1)} %pad_maximum_fusion.12.s3_ref, bf16[64,768]{1,0:T(8,128)(2,1)} %pad_maximum_fusion.19.s2_ref, bf16[32,768]{1,0:T(8,128)(2,1)} %copy-done.8, f32[32,8192]{1,0:T(8,128)} %shard_map.60.refs_0_), custom_call_target="tpu_custom_call" | custom-call | tf_op jit(solution)/shard_map/pallas_call | solution.py:244
  107.9 2.3 fusion.89
  116.9 7.4 %collective-permute-done.5 = f32[33,2048]{1,0:T(8,128)S(1)} collective-permute-done((f32[33,2048]{1,0:T(8,128)S(1)}, f32[33,2048]{1,0:T(8,128)S(1)}, u32[]{:S(2)}, u32[]{:S(2)}) %collective-permute-start.5) | collective-permute-done | bytes 270368 | tf_op jit(solution)/shard_map/ppermute | solution.py:112
  126.9 7.4 %collective-permute-done.6 = f32[33,2048]{1,0:T(8,128)S(1)} collective-permute-done((f32[33,2048]{1,0:T(8,128)S(1)}, f32[33,2048]{1,0:T(8,128)S(1)}, u32[]{:S(2)}, u32[]{:S(2)}) %collective-permute-start.6) | collective-permute-done | bytes 270368 | tf_op jit(solution)/shard_map/ppermute | solution.py:119
  136.5 5.3 %collective-permute-done.10 = f32[8224]{0:T(1024)S(1)} collective-permute-done((f32[8224]{0:T(1024)S(1)}, f32[8224]{0:T(1024)S(1)}, u32[]{:S(2)}, u32[]{:S(2)}) %collective-permute-start.10) | collective-permute-done | bytes 32928 | tf_op jit(solution)/shard_map/ppermute | solution.py:46
  143.3 2.5 collective-permute-done.11
  146.1 3.7 %collective-permute-done.7 = f32[1,32,32]{2,1,0:T(8,128)S(1)} collective-permute-done((f32[1,32,32]{2,1,0:T(8,128)S(1)}, f32[1,32,32]{2,1,0:T(8,128)S(1)}, u32[]{:S(2)}, u32[]{:S(2)}) %collective-permute-start.7) | collective-permute-done | bytes 4128 | tf_op jit(solution)/shard_map/ppermute | solution.py:46
  151.2 3.3 %collective-permute-done.8 = f32[1,32,32]{2,1,0:T(8,128)S(1)} collective-permute-done((f32[1,32,32]{2,1,0:T(8,128)S(1)}, f32[1,32,32]{2,1,0:T(8,128)S(1)}, u32[]{:S(2)}, u32[]{:S(2)}) %collective-permute-start.8) | collective-permute-done | bytes 4128 | tf_op jit(solution)/shard_map/ppermute | solution.py:46
  157.1 3.4 %collective-permute-done.14 = f32[32,32]{0,1:T(8,128)S(1)} collective-permute-done((f32[32,32]{0,1:T(8,128)S(1)}, f32[32,32]{0,1:T(8,128)S(1)}, u32[]{:S(2)}, u32[]{:S(2)}) %collective-permute-start.14) | collective-permute-done | bytes 4128 | tf_op jit(solution)/shard_map/ppermute | solution.py:46
  161.8 3.3 %collective-permute-done.15 = f32[32,32]{0,1:T(8,128)S(1)} collective-permute-done((f32[32,32]{0,1:T(8,128)S(1)}, f32[32,32]{0,1:T(8,128)S(1)}, u32[]{:S(2)}, u32[]{:S(2)}) %collective-permute-start.15) | collective-permute-done | bytes 4128 | tf_op jit(solution)/shard_map/ppermute | solution.py:46
  165.2 2.9 cholesky.70
  169.5 2.4 custom-call.18
  175.7 16.7 %shard_map.62 = f32[768,32]{1,0:T(8,128)} custom-call(f32[1536,8192]{1,0:T(8,128)} %x_ref.15, f32[6,1,8192]{2,1,0:T(1,128)} %broadcast_in_dim_reshape.3.m_ref, bf16[96,8192]{1,0:T(8,128)(2,1)} %pad_maximum_fusion.2.s3_ref, bf16[64,8192]{1,0:T(8,128)(2,1)} %pad_maximum_fusion.5.s2_ref, bf16[32,8192]{1,0:T(8,128)(2,1)} %copy-done.2), custom_call_target="tpu_custom_call" | custom-call | tf_op jit(solution)/shard_map/pallas_call | solution.py:217
  192.3 16.8 %shard_map.63 = f32[768,32]{1,0:T(8,128)} custom-call(f32[1536,8192]{1,0:T(8,128)} %x_ref.15, f32[6,1,8192]{2,1,0:T(1,128)} %broadcast_in_dim_reshape.3.m_ref, bf16[96,8192]{1,0:T(8,128)(2,1)} %pad_maximum_fusion.2.s3_ref, bf16[64,8192]{1,0:T(8,128)(2,1)} %pad_maximum_fusion.5.s2_ref, bf16[32,8192]{1,0:T(8,128)(2,1)} %copy-done.2), custom_call_target="tpu_custom_call" | custom-call | tf_op jit(solution)/shard_map/pallas_call | solution.py:217
  224.9 14.1 %shard_map.64.refs_0_ = f32[32,8192]{1,0:T(8,128)} custom-call(f32[1536,8192]{1,0:T(8,128)} %x_ref.15, f32[6,1,8192]{2,1,0:T(1,128)} %broadcast_in_dim_reshape.3.m_ref, bf16[96,768]{1,0:T(8,128)(2,1)} %pad_maximum_fusion.15.s3_ref, bf16[64,768]{1,0:T(8,128)(2,1)} %pad_maximum_fusion.22.s2_ref, bf16[32,768]{1,0:T(8,128)(2,1)} %copy-done.10), custom_call_target="tpu_custom_call" | custom-call | tf_op jit(solution)/shard_map/pallas_call | solution.py:244
  239.1 14.5 %shard_map.65 = f32[32,8192]{1,0:T(8,128)} custom-call(f32[1536,8192]{1,0:T(8,128)} %x_ref.15, f32[6,1,8192]{2,1,0:T(1,128)} %broadcast_in_dim_reshape.3.m_ref, bf16[96,768]{1,0:T(8,128)(2,1)} %pad_maximum_fusion.14.s3_ref, bf16[64,768]{1,0:T(8,128)(2,1)} %pad_maximum_fusion.21.s2_ref, bf16[32,768]{1,0:T(8,128)(2,1)} %copy-done.9, f32[32,8192]{1,0:T(8,128)} %shard_map.64.refs_0_), custom_call_target="tpu_custom_call" | custom-call | tf_op jit(solution)/shard_map/pallas_call | solution.py:244
  259.8 2.4 collective-permute-done.20
  265.7 8.2 %collective-permute-done.21 = f32[33,2048]{1,0:T(8,128)S(1)} collective-permute-done((f32[33,2048]{1,0:T(8,128)S(1)}, f32[33,2048]{1,0:T(8,128)S(1)}, u32[]{:S(2)}, u32[]{:S(2)}) %collective-permute-start.21) | collective-permute-done | bytes 270368 | tf_op jit(solution)/shard_map/ppermute | solution.py:112
  275.6 7.5 %collective-permute-done.22 = f32[33,2048]{1,0:T(8,128)S(1)} collective-permute-done((f32[33,2048]{1,0:T(8,128)S(1)}, f32[33,2048]{1,0:T(8,128)S(1)}, u32[]{:S(2)}, u32[]{:S(2)}) %collective-permute-start.22) | collective-permute-done | bytes 270368 | tf_op jit(solution)/shard_map/ppermute | solution.py:119
  286.7 3.0 collective-permute-done.25
  292.2 2.7 collective-permute-done.24
  306.8 2.9 cholesky.81
  311.8 2.4 custom-call.19
  (212 shorter events, 94.4 us)
Async XLA Ops:
  6.2 20.0 %copy-start = (f32[8192,32]{0,1:T(8,128)S(1)}, f32[8192,32]{0,1:T(8,128)}, u32[]{:S(2)}) copy-start(f32[8192,32]{0,1:T(8,128)} %param.10) | copy-start | bytes 3145732
  27.5 25.8 %collective-permute-start = (f32[34,768]{1,0:T(8,128)S(1)}, f32[34,768]{1,0:T(8,128)S(1)}, u32[]{:S(2)}, u32[]{:S(2)}) collective-permute-start(f32[34,768]{1,0:T(8,128)S(1)} %pad_maximum_fusion.16), channel_id=1, source_target_pairs={{0,1},{1,0},{2,3},{3,2},{4,5},{5,4},{6,7},{7,6},{8,9},{9,8},{10,11... | collective-permute-start | bytes 313352 | tf_op jit(solution)/shard_map/ppermute | solution.py:46
  53.2 7.5 %collective-permute-start.2 = (f32[33,768]{1,0:T(8,128)S(1)}, f32[33,768]{1,0:T(8,128)S(1)}, u32[]{:S(2)}, u32[]{:S(2)}) collective-permute-start(f32[33,768]{1,0:T(8,128)S(1)} %pad_maximum_fusion.17), channel_id=1, source_target_pairs={{0,1},{1,0},{2,3},{3,2},{4,5},{5,4},{6,7},{7,6},{8,9},{9,8},{10,11... | collective-permute-start | bytes 304136 | tf_op jit(solution)/shard_map/ppermute | solution.py:46
  53.3 14.7 %collective-permute-start.1 = (f32[34,768]{1,0:T(8,128)S(1)}, f32[34,768]{1,0:T(8,128)S(1)}, u32[]{:S(2)}, u32[]{:S(2)}) collective-permute-start(f32[34,768]{1,0:T(8,128)S(1)} %fusion.87), channel_id=1, source_target_pairs={{0,2},{1,3},{2,0},{3,1},{4,6},{5,7},{6,4},{7,5},{8,10},{9,11},{10,... | collective-permute-start | bytes 313352 | tf_op jit(solution)/shard_map/ppermute | solution.py:46
  60.7 7.3 %collective-permute-start.3 = (f32[33,768]{1,0:T(8,128)S(1)}, f32[33,768]{1,0:T(8,128)S(1)}, u32[]{:S(2)}, u32[]{:S(2)}) collective-permute-start(f32[33,768]{1,0:T(8,128)S(1)} %fusion.86), channel_id=1, source_target_pairs={{0,2},{1,3},{2,0},{3,1},{4,6},{5,7},{6,4},{7,5},{8,10},{9,11},{10,... | collective-permute-start | bytes 304136 | tf_op jit(solution)/shard_map/ppermute | solution.py:46
  76.6 16.8 %copy-start.8 = (bf16[32,768]{1,0:T(8,128)(2,1)}, bf16[32,768]{1,0:T(8,128)(2,1)S(1)}, u32[]{:S(2)}) copy-start(bf16[32,768]{1,0:T(8,128)(2,1)S(1)} %get-tuple-element.47.s1_ref) | copy-start | bytes 147460
  110.8 2.2 collective-permute-start.4
  114.5 9.8 %collective-permute-start.5 = (f32[33,2048]{1,0:T(8,128)S(1)}, f32[33,2048]{1,0:T(8,128)S(1)}, u32[]{:S(2)}, u32[]{:S(2)}) collective-permute-start(f32[33,2048]{1,0:T(8,128)S(1)} %pad_maximum_fusion.8), channel_id=1, source_target_pairs={{0,8},{4,12},{8,0},{12,4},{16,24},{20,28},{24,16},{28,20},{1,9},{5... | collective-permute-start | bytes 811016 | tf_op jit(solution)/shard_map/ppermute | solution.py:112
  125.3 9.0 %collective-permute-start.6 = (f32[33,2048]{1,0:T(8,128)S(1)}, f32[33,2048]{1,0:T(8,128)S(1)}, u32[]{:S(2)}, u32[]{:S(2)}) collective-permute-start(f32[33,2048]{1,0:T(8,128)S(1)} %pad_maximum_fusion.9), channel_id=1, source_target_pairs={{0,16},{4,20},{8,24},{12,28},{16,0},{20,4},{24,8},{28,12},{1,17},{... | collective-permute-start | bytes 811016 | tf_op jit(solution)/shard_map/ppermute | solution.py:119
  126.9 9.0 %collective-permute-start.9 = (f32[8224]{0:T(1024)S(1)}, f32[8224]{0:T(1024)S(1)}, u32[]{:S(2)}, u32[]{:S(2)}) collective-permute-start(f32[8224]{0:T(1024)S(1)} %pad_maximum_fusion.23), channel_id=1, source_target_pairs={{0,4},{4,0},{8,12},{12,8},{16,20},{20,16},{24,28},{28,24},{1,5},{5... | collective-permute-start | bytes 98696 | tf_op jit(solution)/shard_map/ppermute | solution.py:46
  134.4 11.5 %collective-permute-start.12 = (f32[32,2048]{1,0:T(8,128)S(1)}, f32[32,2048]{1,0:T(8,128)S(1)}, u32[]{:S(2)}, u32[]{:S(2)}) collective-permute-start(f32[32,2048]{1,0:T(8,128)S(1)} %slice_add_fusion.4), channel_id=1, source_target_pairs={{0,8},{4,12},{8,0},{12,4},{16,24},{20,28},{24,16},{28,20},{1,9},{5... | collective-permute-start | bytes 786440 | tf_op jit(solution)/shard_map/ppermute | solution.py:125
  135.9 5.9 %collective-permute-start.10 = (f32[8224]{0:T(1024)S(1)}, f32[8224]{0:T(1024)S(1)}, u32[]{:S(2)}, u32[]{:S(2)}) collective-permute-start(f32[8224]{0:T(1024)S(1)} %fusion.84), channel_id=1, source_target_pairs={{0,8},{4,12},{8,0},{12,4},{16,24},{20,28},{24,16},{28,20},{1,9},{5... | collective-permute-start | bytes 98696 | tf_op jit(solution)/shard_map/ppermute | solution.py:46
  141.8 4.0 %collective-permute-start.11 = (f32[8224]{0:T(1024)S(1)}, f32[8224]{0:T(1024)S(1)}, u32[]{:S(2)}, u32[]{:S(2)}) collective-permute-start(f32[8224]{0:T(1024)S(1)} %add.188), channel_id=1, source_target_pairs={{0,16},{4,20},{8,24},{12,28},{16,0},{20,4},{24,8},{28,12},{1,17},{... | collective-permute-start | bytes 98696 | tf_op jit(solution)/shard_map/ppermute | solution.py:46
  145.9 8.5 %collective-permute-start.13 = (f32[32,4096]{1,0:T(8,128)S(1)}, f32[32,4096]{1,0:T(8,128)S(1)}, u32[]{:S(2)}, u32[]{:S(2)}) collective-permute-start(f32[32,4096]{1,0:T(8,128)S(1)} %maximum_select_fusion.2), channel_id=1, source_target_pairs={{0,4},{4,0},{8,12},{12,8},{16,20},{20,16},{24,28},{28,24},{1,5},{5... | collective-permute-start | bytes 1572872 | tf_op jit(solution)/shard_map/ppermute | solution.py:125
  146.0 3.8 %collective-permute-start.7 = (f32[1,32,32]{2,1,0:T(8,128)S(1)}, f32[1,32,32]{2,1,0:T(8,128)S(1)}, u32[]{:S(2)}, u32[]{:S(2)}) collective-permute-start(f32[1,32,32]{2,1,0:T(8,128)S(1)} %add_bitcast_fusion), channel_id=1, source_target_pairs={{0,1},{1,0},{2,3},{3,2},{4,5},{5,4},{6,7},{7,6},{8,9},{9,8},{10,11... | collective-permute-start | bytes 12296 | tf_op jit(solution)/shard_map/ppermute | solution.py:46
  149.8 4.6 %collective-permute-start.8 = (f32[1,32,32]{2,1,0:T(8,128)S(1)}, f32[1,32,32]{2,1,0:T(8,128)S(1)}, u32[]{:S(2)}, u32[]{:S(2)}) collective-permute-start(f32[1,32,32]{2,1,0:T(8,128)S(1)} %add.182), channel_id=1, source_target_pairs={{0,2},{1,3},{2,0},{3,1},{4,6},{5,7},{6,4},{7,5},{8,10},{9,11},{10,... | collective-permute-start | bytes 12296 | tf_op jit(solution)/shard_map/ppermute | solution.py:46
  156.7 3.8 %collective-permute-start.14 = (f32[32,32]{0,1:T(8,128)S(1)}, f32[32,32]{0,1:T(8,128)S(1)}, u32[]{:S(2)}, u32[]{:S(2)}) collective-permute-start(f32[32,32]{0,1:T(8,128)S(1)} %fusion.90), channel_id=1, source_target_pairs={{0,1},{1,0},{2,3},{3,2},{4,5},{5,4},{6,7},{7,6},{8,9},{9,8},{10,11... | collective-permute-start | bytes 12296 | tf_op jit(solution)/shard_map/ppermute | solution.py:46
  160.5 4.6 %collective-permute-start.15 = (f32[32,32]{0,1:T(8,128)S(1)}, f32[32,32]{0,1:T(8,128)S(1)}, u32[]{:S(2)}, u32[]{:S(2)}) collective-permute-start(f32[32,32]{0,1:T(8,128)S(1)} %add.191), channel_id=1, source_target_pairs={{0,2},{1,3},{2,0},{3,1},{4,6},{5,7},{6,4},{7,5},{8,10},{9,11},{10,... | collective-permute-start | bytes 12296 | tf_op jit(solution)/shard_map/ppermute | solution.py:46
  209.2 5.6 %collective-permute-start.16 = (f32[32,768]{1,0:T(8,128)S(1)}, f32[32,768]{1,0:T(8,128)S(1)}, u32[]{:S(2)}, u32[]{:S(2)}) collective-permute-start(f32[32,768]{1,0:T(8,128)S(1)} %bitcast.131), channel_id=1, source_target_pairs={{0,1},{1,0},{2,3},{3,2},{4,5},{5,4},{6,7},{7,6},{8,9},{9,8},{10,11... | collective-permute-start | bytes 294920 | tf_op jit(solution)/shard_map/ppermute | solution.py:46
  211.7 6.0 %collective-permute-start.18 = (f32[33,768]{1,0:T(8,128)S(1)}, f32[33,768]{1,0:T(8,128)S(1)}, u32[]{:S(2)}, u32[]{:S(2)}) collective-permute-start(f32[33,768]{1,0:T(8,128)S(1)} %pad_maximum_fusion.18), channel_id=1, source_target_pairs={{0,1},{1,0},{2,3},{3,2},{4,5},{5,4},{6,7},{7,6},{8,9},{9,8},{10,11... | collective-permute-start | bytes 304136 | tf_op jit(solution)/shard_map/ppermute | solution.py:46
  214.8 6.6 %collective-permute-start.17 = (f32[32,768]{1,0:T(8,128)S(1)}, f32[32,768]{1,0:T(8,128)S(1)}, u32[]{:S(2)}, u32[]{:S(2)}) collective-permute-start(f32[32,768]{1,0:T(8,128)S(1)} %bitcast_add_fusion.3), channel_id=1, source_target_pairs={{0,2},{1,3},{2,0},{3,1},{4,6},{5,7},{6,4},{7,5},{8,10},{9,11},{10,... | collective-permute-start | bytes 294920 | tf_op jit(solution)/shard_map/ppermute | solution.py:46
  217.7 5.8 %collective-permute-start.19 = (f32[33,768]{1,0:T(8,128)S(1)}, f32[33,768]{1,0:T(8,128)S(1)}, u32[]{:S(2)}, u32[]{:S(2)}) collective-permute-start(f32[33,768]{1,0:T(8,128)S(1)} %fusion.85), channel_id=1, source_target_pairs={{0,2},{1,3},{2,0},{3,1},{4,6},{5,7},{6,4},{7,5},{8,10},{9,11},{10,... | collective-permute-start | bytes 304136 | tf_op jit(solution)/shard_map/ppermute | solution.py:46
  221.4 17.6 %copy-start.9 = (bf16[32,768]{1,0:T(8,128)(2,1)}, bf16[32,768]{1,0:T(8,128)(2,1)S(1)}, u32[]{:S(2)}) copy-start(bf16[32,768]{1,0:T(8,128)(2,1)S(1)} %get-tuple-element.38.s1_ref) | copy-start | bytes 147460
  259.7 2.4 collective-permute-start.20
  264.1 9.8 %collective-permute-start.21 = (f32[33,2048]{1,0:T(8,128)S(1)}, f32[33,2048]{1,0:T(8,128)S(1)}, u32[]{:S(2)}, u32[]{:S(2)}) collective-permute-start(f32[33,2048]{1,0:T(8,128)S(1)} %pad_maximum_fusion.10), channel_id=1, source_target_pairs={{0,8},{4,12},{8,0},{12,4},{16,24},{20,28},{24,16},{28,20},{1,9},{5... | collective-permute-start | bytes 811016 | tf_op jit(solution)/shard_map/ppermute | solution.py:112
  274.1 9.0 %collective-permute-start.22 = (f32[33,2048]{1,0:T(8,128)S(1)}, f32[33,2048]{1,0:T(8,128)S(1)}, u32[]{:S(2)}, u32[]{:S(2)}) collective-permute-start(f32[33,2048]{1,0:T(8,128)S(1)} %pad_maximum_fusion.11), channel_id=1, source_target_pairs={{0,16},{4,20},{8,24},{12,28},{16,0},{20,4},{24,8},{28,12},{1,17},{... | collective-permute-start | bytes 811016 | tf_op jit(solution)/shard_map/ppermute | solution.py:119
  283.1 6.7 %collective-permute-start.25 = (f32[32,2048]{1,0:T(8,128)S(1)}, f32[32,2048]{1,0:T(8,128)S(1)}, u32[]{:S(2)}, u32[]{:S(2)}) collective-permute-start(f32[32,2048]{1,0:T(8,128)S(1)} %slice_add_fusion.2), channel_id=1, source_target_pairs={{0,8},{4,12},{8,0},{12,4},{16,24},{20,28},{24,16},{28,20},{1,9},{5... | collective-permute-start | bytes 786440 | tf_op jit(solution)/shard_map/ppermute | solution.py:125
  284.8 5.2 %collective-permute-start.23 = (f32[2,32,32]{2,1,0:T(8,128)S(1)}, f32[2,32,32]{2,1,0:T(8,128)S(1)}, u32[]{:S(2)}, u32[]{:S(2)}) collective-permute-start(f32[2,32,32]{2,1,0:T(8,128)S(1)} %add_add_fusion), channel_id=1, source_target_pairs={{0,1},{1,0},{2,3},{3,2},{4,5},{5,4},{6,7},{7,6},{8,9},{9,8},{10,11... | collective-permute-start | bytes 24584 | tf_op jit(solution)/shard_map/ppermute | solution.py:46
  289.8 6.2 %collective-permute-start.26 = (f32[32,4096]{1,0:T(8,128)S(1)}, f32[32,4096]{1,0:T(8,128)S(1)}, u32[]{:S(2)}, u32[]{:S(2)}) collective-permute-start(f32[32,4096]{1,0:T(8,128)S(1)} %maximum_select_fusion.3), channel_id=1, source_target_pairs={{0,4},{4,0},{8,12},{12,8},{16,20},{20,16},{24,28},{28,24},{1,5},{5... | collective-permute-start | bytes 1572872 | tf_op jit(solution)/shard_map/ppermute | solution.py:125
  290.0 4.9 %collective-permute-start.24 = (f32[2,32,32]{2,1,0:T(8,128)S(1)}, f32[2,32,32]{2,1,0:T(8,128)S(1)}, u32[]{:S(2)}, u32[]{:S(2)}) collective-permute-start(f32[2,32,32]{2,1,0:T(8,128)S(1)} %add.204), channel_id=1, source_target_pairs={{0,2},{1,3},{2,0},{3,1},{4,6},{5,7},{6,4},{7,5},{8,10},{9,11},{10,... | collective-permute-start | bytes 24584 | tf_op jit(solution)/shard_map/ppermute | solution.py:46
  298.3 3.8 %collective-permute-start.27 = (f32[32,32]{0,1:T(8,128)S(1)}, f32[32,32]{0,1:T(8,128)S(1)}, u32[]{:S(2)}, u32[]{:S(2)}) collective-permute-start(f32[32,32]{0,1:T(8,128)S(1)} %fusion.91), channel_id=1, source_target_pairs={{0,1},{1,0},{2,3},{3,2},{4,5},{5,4},{6,7},{7,6},{8,9},{9,8},{10,11... | collective-permute-start | bytes 12296 | tf_op jit(solution)/shard_map/ppermute | solution.py:46
  302.1 4.6 %collective-permute-start.28 = (f32[32,32]{0,1:T(8,128)S(1)}, f32[32,32]{0,1:T(8,128)S(1)}, u32[]{:S(2)}, u32[]{:S(2)}) collective-permute-start(f32[32,32]{0,1:T(8,128)S(1)} %add.207), channel_id=1, source_target_pairs={{0,2},{1,3},{2,0},{3,1},{4,6},{5,7},{6,4},{7,5},{8,10},{9,11},{10,... | collective-permute-start | bytes 12296 | tf_op jit(solution)/shard_map/ppermute | solution.py:46
  (10 other events, 32.9 us)
